TPU v7x, 256 devices: a whole 4x4x8 slice. The times are simulated.
256 devices in a mesh: ctx: 16 (over z, core), head: 16 (over y, x).
Axes of the slice: x: 4, y: 4, z: 8, core: 2. Of those that a mesh axis runs over, the one named last changes fastest.
Arguments:
- x_proj: bfloat16 [8192, 8192], P('ctx', 'head'), may hold values from -6 to 6
- z_proj: bfloat16 [8192, 8192], P('ctx', 'head'), may hold values from -6 to 6
- b_proj: bfloat16 [8192, 128], P('ctx'), may hold values from -6 to 6
- c_proj: bfloat16 [8192, 128], P('ctx'), may hold values from -6 to 6
- dt_raw: float32 [128, 8192], P('head', 'ctx'), may hold values from -6 to -2
- a_log: float32 [128], P('head'), may hold values from -11 to 4
- d_skip: float32 [128], P('head'), may hold values from 0.5 to 2
- conv_x: float32 [4, 8192], P(None, 'head'), may hold values from -3 to 3
- conv_bc: float32 [4, 256], replicated, may hold values from -3 to 3
- norm_gain: float32 [8192], P('head'), may hold values from 0.5 to 1.5
- grad_out: bfloat16 [8192, 8192], P('ctx', 'head'), may hold values from -6 to 6
Outputs:
- y_out: bfloat16 [8192, 8192], P('ctx', 'head')
- grad_x: bfloat16 [8192, 8192], P('ctx', 'head')
- grad_z: bfloat16 [8192, 8192], P('ctx', 'head')
- grad_b: bfloat16 [8192, 128], P(('ctx', 'head'))
- grad_c: bfloat16 [8192, 128], P(('ctx', 'head'))
- grad_dt: float32 [128, 8192], P('head', 'ctx')
- grad_alog: float32 [128], P('head')
- grad_dskip: float32 [128], P('head')
- grad_convx: float32 [4, 8192], P(None, 'head')
- grad_convbc: float32 [4, 256], replicated
- grad_gain: float32 [8192], P('head')
All inputs are finite; a program needn't handle non-finite values.
Results may differ from a plain program's by a relative error of at most 0.023.
Values may be sent and summed in bfloat16 or wider, within the bound.
No kernel may reach another device: no remote copies, remote signals or barrier semaphores. Data moves between devices by JAX's collectives and lax.ppermute only.
A program may use at most 64 MiB of HBM per device.

v0:
```python
import jax
import jax.numpy as jnp
from jax import lax
from jax.sharding import PartitionSpec as P

HEADS = 128
HEAD_DIM = 64
GROUP = 256
HIGH = lax.Precision.HIGHEST
EPS = 1e-05


def passed_along(block, axis, distance):
    devices = range(lax.axis_size(axis))
    route = [(i - distance, i) for i in devices if i - distance in devices]
    return lax.ppermute(block, axis, route)


def silu_grad(value):
    sigma = jax.nn.sigmoid(value)
    return sigma * (1.0 + value * (1.0 - sigma))


def tap_sum(padded, weight, count):
    summed = jnp.zeros((count, padded.shape[1]), jnp.float32)
    for offset in range(weight.shape[0]):
        summed = summed + weight[offset][None, :] * padded[offset : offset + count].astype(
            jnp.float32
        )
    return summed


def back_taps(ahead, weight, count):
    final_tap = weight.shape[0] - 1
    summed = jnp.zeros((count, ahead.shape[1]), jnp.float32)
    for offset in range(weight.shape[0]):
        summed = (
            summed
            + weight[offset][None, :] * ahead[final_tap - offset : final_tap - offset + count]
        )
    return summed


def weight_taps(grad_pre, padded, count, tap_count):
    return jnp.stack(
        [
            jnp.sum(grad_pre * padded[offset : offset + count].astype(jnp.float32), axis=0)
            for offset in range(tap_count)
        ]
    )


def decay_table(cum_here):
    size_rows = cum_here.shape[0]
    row_ids = lax.broadcasted_iota(jnp.int32, (size_rows, size_rows), 0)
    col_ids = lax.broadcasted_iota(jnp.int32, (size_rows, size_rows), 1)
    allowed = (col_ids <= row_ids)[:, :, None]
    spread = cum_here[:, None, :] - cum_here[None, :, :]
    return jnp.where(allowed, jnp.exp(jnp.where(allowed, spread, 0.0)), 0.0)


def local(
    x_proj, z_proj, b_proj, c_proj, dt_raw, a_log, d_skip, conv_x, conv_bc, norm_gain, grad_out
):
    length = x_proj.shape[0]
    head_count = dt_raw.shape[0]
    row_width = x_proj.shape[1]
    head_dim = row_width // head_count
    state_dim = b_proj.shape[1]
    tap_count = conv_x.shape[0]
    blocks = length // GROUP
    channels = HEADS * HEAD_DIM
    bc_proj = jnp.concatenate([b_proj, c_proj], axis=1)
    edges = passed_along(
        (x_proj[length - tap_count + 1 :], bc_proj[length - tap_count + 1 :]), "ctx", 1
    )
    x_padded = jnp.concatenate([edges[0], x_proj], axis=0)
    bc_padded = jnp.concatenate([edges[1], bc_proj], axis=0)
    x_pre = tap_sum(x_padded, conv_x, length)
    bc_pre = tap_sum(bc_padded, conv_bc, length)
    x_act = jax.nn.silu(x_pre)
    bc_act = jax.nn.silu(bc_pre)
    decay_rate = jnp.exp(a_log)
    step_size = jax.nn.softplus(dt_raw).T
    x_blocks = x_act.reshape(blocks, GROUP, head_count, head_dim)
    b_blocks = bc_act[:, :state_dim].reshape(blocks, GROUP, state_dim)
    c_blocks = bc_act[:, state_dim:].reshape(blocks, GROUP, state_dim)
    d_blocks = step_size.reshape(blocks, GROUP, head_count)
    cum_blocks = jnp.cumsum(
        (-step_size * decay_rate[None, :]).reshape(blocks, GROUP, head_count), axis=1
    )
    block_ends = cum_blocks[:, -1, :]
    block_decay = jnp.exp(block_ends)
    tail_weight = jnp.exp(cum_blocks[:, -1:, :] - cum_blocks) * d_blocks
    block_states = jnp.einsum(
        "cshp,csn->chpn", tail_weight[..., None] * x_blocks, b_blocks, precision=HIGH
    )

    def fold_blocks(running, inputs):
        decay_now, state_now = inputs
        return (decay_now[:, None, None] * running + state_now, running)

    empty_state = jnp.zeros((head_count, head_dim, state_dim), jnp.float32)
    shard_state, local_entering = lax.scan(fold_blocks, empty_state, (block_decay, block_states))
    prefix_log = jnp.cumsum(block_ends, axis=0) - block_ends
    shard_decay = jnp.exp(jnp.sum(block_ends, axis=0))

    def pass_on(step_index, incoming):
        outgoing = shard_decay[:, None, None] * incoming + shard_state
        return passed_along(outgoing, "ctx", 1)

    entering = lax.fori_loop(0, lax.axis_size("ctx") - 1, pass_on, empty_state)
    block_entry = jnp.exp(prefix_log)[:, :, None, None] * entering[None] + local_entering

    def forward_block(inputs):
        x_here, b_here, c_here, d_here, cum_here, entry = inputs
        decay_map = decay_table(cum_here)
        scores = jnp.dot(c_here, b_here.T, precision=HIGH)
        mixing = scores[:, :, None] * decay_map * d_here[None, :, :]
        inside = jnp.einsum("tsh,shp->thp", mixing, x_here, precision=HIGH)
        carried = jnp.exp(cum_here)[:, :, None] * jnp.einsum(
            "tn,hpn->thp", c_here, entry, precision=HIGH
        )
        return inside + carried

    ssm_blocks = lax.map(
        forward_block, (x_blocks, b_blocks, c_blocks, d_blocks, cum_blocks, block_entry)
    )
    skip_rep = jnp.repeat(d_skip, head_dim)
    ssm_out = ssm_blocks.reshape(length, row_width) + skip_rep[None, :] * x_act
    z_float = z_proj.astype(jnp.float32)
    gate_act = jax.nn.silu(z_float)
    gated_out = ssm_out * gate_act
    grad_float = grad_out.astype(jnp.float32)
    scaled_grad = norm_gain[None, :] * grad_float
    square_sum, cross_sum = lax.psum(
        (jnp.sum(gated_out * gated_out, axis=1), jnp.sum(scaled_grad * gated_out, axis=1)), "head"
    )
    inv_rms = lax.rsqrt(square_sum / channels + EPS)[:, None]
    y_out = (gated_out * inv_rms * norm_gain[None, :]).astype(jnp.bfloat16)
    grad_gain_part = jnp.sum(grad_float * gated_out * inv_rms, axis=0)
    grad_gated = inv_rms * scaled_grad - gated_out * (inv_rms * inv_rms * inv_rms) * (
        cross_sum[:, None] / channels
    )
    grad_ssm = grad_gated * gate_act
    grad_z = (grad_gated * ssm_out * silu_grad(z_float)).astype(jnp.bfloat16)
    grad_skip_part = jnp.sum((grad_ssm * x_act).reshape(length, head_count, head_dim), axis=(0, 2))
    grad_blocks = grad_ssm.reshape(blocks, GROUP, head_count, head_dim)
    local_pull = jnp.einsum(
        "cthp,ctn->chpn", jnp.exp(cum_blocks)[..., None] * grad_blocks, c_blocks, precision=HIGH
    )
    shard_pull = jnp.sum(jnp.exp(prefix_log)[:, :, None, None] * local_pull, axis=0)

    def pass_back(step_index, incoming):
        outgoing = shard_decay[:, None, None] * incoming + shard_pull
        return passed_along(outgoing, "ctx", -1)

    leaving = lax.fori_loop(0, lax.axis_size("ctx") - 1, pass_back, empty_state)
    _, block_exit = lax.scan(fold_blocks, leaving, (block_decay, local_pull), reverse=True)

    def backward_block(inputs):
        x_here, b_here, c_here, d_here, cum_here, entry, exit_grad, grad_here = inputs
        decay_map = decay_table(cum_here)
        scores = jnp.dot(c_here, b_here.T, precision=HIGH)
        weighted = scores[:, :, None] * decay_map
        tail_decay = jnp.exp(cum_here[-1:, :] - cum_here)
        b_exit = jnp.einsum("sn,hpn->shp", b_here, exit_grad, precision=HIGH)
        pulled = (
            jnp.einsum("tsh,thp->shp", weighted, grad_here, precision=HIGH)
            + tail_decay[:, :, None] * b_exit
        )
        grad_x_here = d_here[:, :, None] * pulled
        grad_step = jnp.sum(x_here * pulled, axis=2)
        pair_grad = jnp.einsum("thp,shp->tsh", grad_here, x_here, precision=HIGH)
        masked = pair_grad * decay_map * d_here[None, :, :]
        grad_scores = jnp.sum(masked, axis=2)
        grad_c_here = jnp.dot(grad_scores, b_here, precision=HIGH)
        grad_b_here = jnp.dot(grad_scores.T, c_here, precision=HIGH)
        through = masked * scores[:, :, None]
        grad_cum = jnp.sum(through, axis=1) - jnp.sum(through, axis=0)
        start_map = jnp.exp(cum_here)[:, :, None] * grad_here
        carried = jnp.einsum("tn,hpn->thp", c_here, entry, precision=HIGH)
        grad_cum = grad_cum + jnp.sum(start_map * carried, axis=2)
        grad_c_here = grad_c_here + jnp.einsum("thp,hpn->tn", start_map, entry, precision=HIGH)
        release = tail_decay * d_here * jnp.sum(x_here * b_exit, axis=2)
        grad_cum = grad_cum - release
        end_total = jnp.sum(release, axis=0) + jnp.exp(cum_here[-1]) * jnp.sum(
            entry * exit_grad, axis=(1, 2)
        )
        grad_cum = jnp.concatenate([grad_cum[:-1], grad_cum[-1:] + end_total[None, :]], axis=0)
        grad_log = jnp.flip(jnp.cumsum(jnp.flip(grad_cum, 0), axis=0), 0)
        grad_b_here = grad_b_here + jnp.einsum(
            "shp,hpn->sn", (tail_decay * d_here)[:, :, None] * x_here, exit_grad, precision=HIGH
        )
        return (grad_x_here, grad_b_here, grad_c_here, grad_step, grad_log)

    grad_x_blocks, grad_b_blocks, grad_c_blocks, grad_step_blocks, grad_log_blocks = lax.map(
        backward_block,
        (x_blocks, b_blocks, c_blocks, d_blocks, cum_blocks, block_entry, block_exit, grad_blocks),
    )
    grad_log_rows = grad_log_blocks.reshape(length, head_count)
    grad_step_rows = (
        grad_step_blocks.reshape(length, head_count) - decay_rate[None, :] * grad_log_rows
    )
    grad_alog_part = decay_rate * -jnp.sum(step_size * grad_log_rows, axis=0)
    grad_dt = (grad_step_rows * jax.nn.sigmoid(dt_raw).T).T
    grad_x_act = grad_x_blocks.reshape(length, row_width) + skip_rep[None, :] * grad_ssm
    grad_bc_act = jnp.concatenate(
        [grad_b_blocks.reshape(length, state_dim), grad_c_blocks.reshape(length, state_dim)], axis=1
    )
    grad_x_pre = grad_x_act * silu_grad(x_pre)
    grad_bc_pre = grad_bc_act * silu_grad(bc_pre)
    ahead = passed_along((grad_x_pre[: tap_count - 1], grad_bc_pre[: tap_count - 1]), "ctx", -1)
    x_ahead = jnp.concatenate([grad_x_pre, ahead[0]], axis=0)
    bc_ahead = jnp.concatenate([grad_bc_pre, ahead[1]], axis=0)
    grad_x = back_taps(x_ahead, conv_x, length).astype(jnp.bfloat16)
    bc_back = back_taps(bc_ahead, conv_bc, length)
    shares = lax.psum_scatter(bc_back, "head", scatter_dimension=0, tiled=True)
    grad_b = shares[:, :state_dim].astype(jnp.bfloat16)
    grad_c = shares[:, state_dim:].astype(jnp.bfloat16)
    grad_convx_part = weight_taps(grad_x_pre, x_padded, length, tap_count)
    grad_convbc_part = weight_taps(grad_bc_pre, bc_padded, length, tap_count)
    grad_alog, grad_dskip, grad_convx, grad_gain = lax.psum(
        (grad_alog_part, grad_skip_part, grad_convx_part, grad_gain_part), "ctx"
    )
    grad_convbc = lax.psum(grad_convbc_part, ("ctx", "head"))
    return (
        y_out,
        grad_x,
        grad_z,
        grad_b,
        grad_c,
        grad_dt,
        grad_alog,
        grad_dskip,
        grad_convx,
        grad_convbc,
        grad_gain,
    )


def solution(mesh):
    return jax.shard_map(
        local,
        mesh=mesh,
        in_specs=(
            P("ctx", "head"),
            P("ctx", "head"),
            P("ctx", None),
            P("ctx", None),
            P("head", "ctx"),
            P("head"),
            P("head"),
            P(None, "head"),
            P(),
            P("head"),
            P("ctx", "head"),
        ),
        out_specs=(
            P("ctx", "head"),
            P("ctx", "head"),
            P("ctx", "head"),
            P(("ctx", "head"), None),
            P(("ctx", "head"), None),
            P("head", "ctx"),
            P("head"),
            P("head"),
            P(None, "head"),
            P(),
            P("head"),
        ),
        check_vma=False,
    )
```

profile of v0, /device:TPU:1, one launch (start us, length us, event | category | flops | bytes accessed | tf_op | source)
XLA Modules:
  0.0 672.7 jit_solution(3489720683614918270)
XLA Ops:
  8.2 4.9 collective-permute-start.2
  35.6 116.3 %while.77 = (s32[]{:T(128)}, f32[8,64,128]{2,1,0:T(8,128)S(1)}, f32[8]{0:T(128)S(1)}, f32[8,64,128]{2,1,0:T(8,128)S(1)}, s32[]{:T(128)}) while((s32[]{:T(128)}, f32[8,64,128]{2,1,0:T(8,128)S(1)}, f32[8]{0:T(128)S(1)}, f32[8,64,128]{2,1,0:T(8,128)S(1)}, s32[]{:T(128)}) %tuple.173), condition=%wide.region_7.8_spmd, body=%wide.region_6.7_spmd.sunk | while | flops 131074 | bytes 1835141 | solution.py:112
  35.7 3.9 collective-permute-start
  39.7 3.3 collective-permute-done
  43.0 4.4 collective-permute-start
  47.4 3.3 collective-permute-done
  50.8 4.4 collective-permute-start
  55.2 3.3 collective-permute-done
  58.6 4.4 collective-permute-start
  63.0 3.3 collective-permute-done
  66.4 4.4 collective-permute-start
  70.8 3.3 collective-permute-done
  74.2 4.4 collective-permute-start
  78.6 3.3 collective-permute-done
  82.0 4.4 collective-permute-start
  89.8 4.4 collective-permute-start
  97.5 4.4 collective-permute-start
  102.0 3.3 collective-permute-done
  105.3 4.4 collective-permute-start
  109.7 3.3 collective-permute-done
  113.1 4.4 collective-permute-start
  117.5 3.3 collective-permute-done
  120.9 4.4 collective-permute-start
  128.7 4.4 collective-permute-start
  133.1 3.3 collective-permute-done
  136.5 4.4 collective-permute-start
  140.9 3.3 collective-permute-done
  144.3 4.4 collective-permute-start
  148.7 3.3 collective-permute-done
  153.4 36.2 %while.78 = (s32[]{:T(128)}, f32[2,256,8,64]{1,0,3,2:T(2,128)}, f32[2,256,8,64]{1,3,2,0:T(8,128)}, f32[2,256,128]{2,1,0:T(8,128)S(1)}, f32[2,256,128]{2,1,0:T(8,...) while((s32[]{:T(128)}, f32[2,256,8,64]{1,0,3,2:T(2,128)}, ...), condition=%wide.region_9.10_spmd, body=%wide.region_8.9_spmd.sunk | while | flops 707592192 | bytes 5580925 | solution.py:126
  155.3 3.6 fusion.217
  160.0 11.5 %dynamic_update_slice.48 = f32[2,256,8,64]{1,0,3,2:T(2,128)} dynamic-update-slice(f32[2,256,8,64]{1,0,3,2:T(2,128)} %get-tuple-element.953, f32[1,256,8,64]{1,0,3,2:T(1,128)S(1)} %copy.218, s32[]{:T(128)S(6)} %copy.254, s32[]{:T(128)} %constant.125.clone.1..sunk, s32[]{:T(128)} %constant.125.clone.1..sunk, s32[]{:T(128)} %constant.125.clone.1..sunk) | dynamic-update-slice | bytes 1048580 | tf_op jit(solution)/shard_map/while/body/jit(dynamic_update_index_in_dim)/dynamic_update_slice | solution.py:126
  173.4 3.6 fusion.217
  178.1 11.5 %dynamic_update_slice.48 = f32[2,256,8,64]{1,0,3,2:T(2,128)} dynamic-update-slice(f32[2,256,8,64]{1,0,3,2:T(2,128)} %get-tuple-element.953, f32[1,256,8,64]{1,0,3,2:T(1,128)S(1)} %copy.218, s32[]{:T(128)S(6)} %copy.254, s32[]{:T(128)} %constant.125.clone.1..sunk, s32[]{:T(128)} %constant.125.clone.1..sunk, s32[]{:T(128)} %constant.125.clone.1..sunk) | dynamic-update-slice | bytes 1048580 | tf_op jit(solution)/shard_map/while/body/jit(dynamic_update_index_in_dim)/dynamic_update_slice | solution.py:126
  192.0 33.5 %psum.49 = f32[512]{0:T(512)S(1)} all-reduce(f32[512]{0:T(512)S(1)} %get-tuple-element.601), channel_id=1, replica_groups=mesh['ctx'=16,'head'=16] {'head'}, use_global_device_ids=true, to_apply=%region_11.12 | all-reduce | flops 512 | bytes 4096 | tf_op jit(solution)/shard_map/psum | solution.py:136
  227.5 28.9 %psum.50 = f32[512]{0:T(512)S(1)} all-reduce(f32[512]{0:T(512)S(1)} %get-tuple-element.496), channel_id=1, replica_groups=mesh['ctx'=16,'head'=16] {'head'}, use_global_device_ids=true, to_apply=%region_13.14 | all-reduce | flops 512 | bytes 4096 | tf_op jit(solution)/shard_map/psum | solution.py:136
  256.4 4.5 multiply_reduce_fusion.3
  263.5 146.2 %while.79 = (s32[]{:T(128)}, f32[8,64,128]{2,1,0:T(8,128)S(1)}, f32[8]{0:T(128)S(1)}, f32[8,64,128]{2,1,0:T(8,128)S(1)}, s32[]{:T(128)}) while((s32[]{:T(128)}, f32[8,64,128]{2,1,0:T(8,128)S(1)}, f32[8]{0:T(128)S(1)}, f32[8,64,128]{2,1,0:T(8,128)S(1)}, s32[]{:T(128)}) %tuple.195), condition=%wide.region_16.17_spmd, body=%wide.region_15.16_spmd.sunk | while | flops 131074 | bytes 1835141 | solution.py:158
  263.6 11.7 %collective-permute-start.1 = (f32[8,64,128]{2,1,0:T(8,128)S(1)}, f32[8,64,128]{2,1,0:T(8,128)S(1)}, u32[]{:S(2)}, u32[]{:S(2)}) collective-permute-start(f32[8,64,128]{2,1,0:T(8,128)S(1)} %multiply_add_fusion.7), channel_id=1, source_target_pairs={{16,0},{32,16},{48,32},{64,48},{80,64},{96,80},{112,96},{128,112},... | collective-permute-start | bytes 786440 | tf_op jit(solution)/shard_map/while/body/eval_jaxpr/ppermute | solution.py:16
  275.3 10.6 %collective-permute-done.1 = f32[8,64,128]{2,1,0:T(8,128)S(1)} collective-permute-done((f32[8,64,128]{2,1,0:T(8,128)S(1)}, f32[8,64,128]{2,1,0:T(8,128)S(1)}, u32[]{:S(2)}, u32[]{:S(2)}) %collective-permute-start.1) | collective-permute-done | bytes 262176 | tf_op jit(solution)/shard_map/while/body/eval_jaxpr/ppermute | solution.py:16
  287.9 5.8 collective-permute-done.1
  295.7 5.8 collective-permute-done.1
  303.5 5.8 collective-permute-done.1
  311.3 7.8 %collective-permute-done.1 = f32[8,64,128]{2,1,0:T(8,128)S(1)} collective-permute-done((f32[8,64,128]{2,1,0:T(8,128)S(1)}, f32[8,64,128]{2,1,0:T(8,128)S(1)}, u32[]{:S(2)}, u32[]{:S(2)}) %collective-permute-start.1) | collective-permute-done | bytes 262176 | tf_op jit(solution)/shard_map/while/body/eval_jaxpr/ppermute | solution.py:16
  321.1 5.8 collective-permute-done.1
  328.9 8.8 %collective-permute-done.1 = f32[8,64,128]{2,1,0:T(8,128)S(1)} collective-permute-done((f32[8,64,128]{2,1,0:T(8,128)S(1)}, f32[8,64,128]{2,1,0:T(8,128)S(1)}, u32[]{:S(2)}, u32[]{:S(2)}) %collective-permute-start.1) | collective-permute-done | bytes 262176 | tf_op jit(solution)/shard_map/while/body/eval_jaxpr/ppermute | solution.py:16
  339.7 7.0 %collective-permute-done.1 = f32[8,64,128]{2,1,0:T(8,128)S(1)} collective-permute-done((f32[8,64,128]{2,1,0:T(8,128)S(1)}, f32[8,64,128]{2,1,0:T(8,128)S(1)}, u32[]{:S(2)}, u32[]{:S(2)}) %collective-permute-start.1) | collective-permute-done | bytes 262176 | tf_op jit(solution)/shard_map/while/body/eval_jaxpr/ppermute | solution.py:16
  348.7 7.0 %collective-permute-done.1 = f32[8,64,128]{2,1,0:T(8,128)S(1)} collective-permute-done((f32[8,64,128]{2,1,0:T(8,128)S(1)}, f32[8,64,128]{2,1,0:T(8,128)S(1)}, u32[]{:S(2)}, u32[]{:S(2)}) %collective-permute-start.1) | collective-permute-done | bytes 262176 | tf_op jit(solution)/shard_map/while/body/eval_jaxpr/ppermute | solution.py:16
  357.7 7.0 %collective-permute-done.1 = f32[8,64,128]{2,1,0:T(8,128)S(1)} collective-permute-done((f32[8,64,128]{2,1,0:T(8,128)S(1)}, f32[8,64,128]{2,1,0:T(8,128)S(1)}, u32[]{:S(2)}, u32[]{:S(2)}) %collective-permute-start.1) | collective-permute-done | bytes 262176 | tf_op jit(solution)/shard_map/while/body/eval_jaxpr/ppermute | solution.py:16
  366.7 7.0 %collective-permute-done.1 = f32[8,64,128]{2,1,0:T(8,128)S(1)} collective-permute-done((f32[8,64,128]{2,1,0:T(8,128)S(1)}, f32[8,64,128]{2,1,0:T(8,128)S(1)}, u32[]{:S(2)}, u32[]{:S(2)}) %collective-permute-start.1) | collective-permute-done | bytes 262176 | tf_op jit(solution)/shard_map/while/body/eval_jaxpr/ppermute | solution.py:16
  375.7 7.0 %collective-permute-done.1 = f32[8,64,128]{2,1,0:T(8,128)S(1)} collective-permute-done((f32[8,64,128]{2,1,0:T(8,128)S(1)}, f32[8,64,128]{2,1,0:T(8,128)S(1)}, u32[]{:S(2)}, u32[]{:S(2)}) %collective-permute-start.1) | collective-permute-done | bytes 262176 | tf_op jit(solution)/shard_map/while/body/eval_jaxpr/ppermute | solution.py:16
  384.7 7.0 %collective-permute-done.1 = f32[8,64,128]{2,1,0:T(8,128)S(1)} collective-permute-done((f32[8,64,128]{2,1,0:T(8,128)S(1)}, f32[8,64,128]{2,1,0:T(8,128)S(1)}, u32[]{:S(2)}, u32[]{:S(2)}) %collective-permute-start.1) | collective-permute-done | bytes 262176 | tf_op jit(solution)/shard_map/while/body/eval_jaxpr/ppermute | solution.py:16
  393.7 7.0 %collective-permute-done.1 = f32[8,64,128]{2,1,0:T(8,128)S(1)} collective-permute-done((f32[8,64,128]{2,1,0:T(8,128)S(1)}, f32[8,64,128]{2,1,0:T(8,128)S(1)}, u32[]{:S(2)}, u32[]{:S(2)}) %collective-permute-start.1) | collective-permute-done | bytes 262176 | tf_op jit(solution)/shard_map/while/body/eval_jaxpr/ppermute | solution.py:16
  402.7 7.0 %collective-permute-done.1 = f32[8,64,128]{2,1,0:T(8,128)S(1)} collective-permute-done((f32[8,64,128]{2,1,0:T(8,128)S(1)}, f32[8,64,128]{2,1,0:T(8,128)S(1)}, u32[]{:S(2)}, u32[]{:S(2)}) %collective-permute-start.1) | collective-permute-done | bytes 262176 | tf_op jit(solution)/shard_map/while/body/eval_jaxpr/ppermute | solution.py:16
  411.4 87.2 %while.81 = (s32[]{:T(128)}, f32[2,256,8,64]{1,0,3,2:T(2,128)}, f32[2,256,128]{2,1,0:T(8,128)}, f32[2,256,128]{2,1,0:T(8,128)}, f32[2,256,8]{1,2,0:T(8,128)}, /*...) while((s32[]{:T(128)}, f32[2,256,8,64]{1,0,3,2:T(2,128)}, ...), condition=%wide.region_30.31_spmd, body=%wide.region_19.30_spmd.sunk | while | flops 1921460224 | bytes 14728557 | solution.py:197
  417.7 4.2 fusion.237
  423.3 4.3 multiply_reduce_fusion.9
  443.5 11.5 %dynamic_update_slice.53 = f32[2,256,8,64]{1,0,3,2:T(2,128)} dynamic-update-slice(f32[2,256,8,64]{1,0,3,2:T(2,128)} %get-tuple-element.1024, f32[1,256,8,64]{1,0,3,2:T(1,128)S(1)} %copy.224, s32[]{:T(128)S(6)} %copy.279, s32[]{:T(128)} %constant.125.clone.1..sunk.1, s32[]{:T(128)} %constant.125.clone.1..sunk.1, s32[]{:T(128)} %constant.125.clone.1..sunk.1) | dynamic-update-slice | bytes 1048580 | tf_op jit(solution)/shard_map/while/body/jit(dynamic_update_index_in_dim)/dynamic_update_slice | solution.py:126
  461.3 4.2 fusion.237
  466.9 4.3 multiply_reduce_fusion.9
  487.1 11.5 %dynamic_update_slice.53 = f32[2,256,8,64]{1,0,3,2:T(2,128)} dynamic-update-slice(f32[2,256,8,64]{1,0,3,2:T(2,128)} %get-tuple-element.1024, f32[1,256,8,64]{1,0,3,2:T(1,128)S(1)} %copy.224, s32[]{:T(128)S(6)} %copy.279, s32[]{:T(128)} %constant.125.clone.1..sunk.1, s32[]{:T(128)} %constant.125.clone.1..sunk.1, s32[]{:T(128)} %constant.125.clone.1..sunk.1) | dynamic-update-slice | bytes 1048580 | tf_op jit(solution)/shard_map/while/body/jit(dynamic_update_index_in_dim)/dynamic_update_slice | solution.py:126
  508.5 3.8 fusion.109
  515.5 62.7 %all-reduce = (f32[8]{0:T(128)}, f32[8]{0:T(128)}, f32[4,512]{1,0:T(4,128)}, f32[512]{0:T(512)}) all-reduce(f32[8]{0:T(128)S(1)} %negate_multiply_fusion, f32[8]{0:T(128)S(1)} %reduce_sum.225, f32[4,512]{1,0:T(4,128)S(1)} %pad_maximum_fusion.5, f32[512]{0:T(512)S(1)} %copy-done.40), channel_id=1, replica_groups=mesh['ctx'=16,'head'=16] {'ctx'}, use_global_device_ids=true, to_apply=%region_33.34 | all-reduce | flops 2576 | bytes 20608 | tf_op jit(solution)/shard_map/psum | solution.py:223
  581.2 80.8 %psum.54 = f32[4,256]{1,0:T(4,128)} all-reduce(f32[4,256]{1,0:T(4,128)S(1)} %pad_maximum_fusion.6), channel_id=1, replica_groups=mesh['ctx'=16,'head'=16] {'ctx','head'}, use_global_device_ids=true, to_apply=%region_46.47 | all-reduce | flops 1024 | bytes 8192 | tf_op jit(solution)/shard_map/psum | solution.py:226
  (308 shorter events, 145.9 us)
Async XLA Ops:
  7.2 18.2 %copy-start.11 = (bf16[512,512]{1,0:T(8,128)(2,1)S(1)}, bf16[512,512]{1,0:T(8,128)(2,1)}, u32[]{:S(2)}) copy-start(bf16[512,512]{1,0:T(8,128)(2,1)} %param.23) | copy-start | bytes 1572868
  7.2 18.4 %copy-start.43 = (f32[8]{0:T(128)S(1)}, f32[8]{0:T(128)}, u32[]{:S(2)}) copy-start(f32[8]{0:T(128)} %param.29) | copy-start | bytes 100
  7.2 657.3 %reduce-scatter.2.cloned.1.call-start = ((), (), s32[]{:S(2)}) async-start(), calls=%async_computation.1 | async-start | bytes 557056 | tf_op jit(solution)/shard_map/reduce_scatter | solution.py:218
  8.0 17.9 %copy-start.12 = (bf16[512,512]{1,0:T(8,128)(2,1)S(1)}, bf16[512,512]{1,0:T(8,128)(2,1)}, u32[]{:S(2)}) copy-start(bf16[512,512]{1,0:T(8,128)(2,1)} %param.24) | copy-start | bytes 1572868
  8.2 20.1 %collective-permute-start.2 = (bf16[3,512]{0,1:T(8,128)(2,1)S(1)}, bf16[3,512]{0,1:T(8,128)(2,1)S(1)}, u32[]{:S(2)}, u32[]{:S(2)}) collective-permute-start(bf16[3,512]{0,1:T(8,128)(2,1)S(1)} %copy.135), channel_id=1, source_target_pairs={{0,16},{16,32},{32,48},{48,64},{64,80},{80,96},{96,112},{112,128},... | collective-permute-start | bytes 9224 | tf_op jit(solution)/shard_map/ppermute | solution.py:16
  15.0 12.9 %copy-start.10 = (bf16[512,256]{1,0:T(8,128)(2,1)}, bf16[512,256]{1,0:T(8,128)(2,1)S(1)}, u32[]{:S(2)}) copy-start(bf16[512,256]{1,0:T(8,128)(2,1)S(1)} %constant_dynamic-update-slice_fusion) | copy-start | bytes 786436
  15.0 12.9 %collective-permute-start.3 = (bf16[3,256]{1,0:T(4,128)(2,1)S(1)}, bf16[3,256]{1,0:T(4,128)(2,1)S(1)}, u32[]{:S(2)}, u32[]{:S(2)}) collective-permute-start(bf16[3,256]{1,0:T(4,128)(2,1)S(1)} %slice.165), channel_id=1, source_target_pairs={{0,16},{16,32},{32,48},{48,64},{64,80},{80,96},{96,112},{112,128},... | collective-permute-start | bytes 4616 | tf_op jit(solution)/shard_map/ppermute | solution.py:16
  18.4 9.4 %copy-start.29 = (f32[1,256]{1,0:T(1,128)}, f32[1,256]{1,0:T(1,128)S(1)}, u32[]{:S(2)}) copy-start(f32[1,256]{1,0:T(1,128)S(1)} %get-tuple-element.620) | copy-start | bytes 3076
  18.4 9.4 %copy-start.31 = (f32[1,256]{1,0:T(1,128)}, f32[1,256]{1,0:T(1,128)S(1)}, u32[]{:S(2)}) copy-start(f32[1,256]{1,0:T(1,128)S(1)} %get-tuple-element.621) | copy-start | bytes 3076
  18.4 9.4 %copy-start.33 = (f32[1,256]{1,0:T(1,128)}, f32[1,256]{1,0:T(1,128)S(1)}, u32[]{:S(2)}) copy-start(f32[1,256]{1,0:T(1,128)S(1)} %get-tuple-element.622) | copy-start | bytes 3076
  18.5 9.4 %copy-start.35 = (f32[1,256]{1,0:T(1,128)}, f32[1,256]{1,0:T(1,128)S(1)}, u32[]{:S(2)}) copy-start(f32[1,256]{1,0:T(1,128)S(1)} %get-tuple-element.623) | copy-start | bytes 3076
  19.3 9.0 %copy-start.19 = (f32[1,512]{1,0:T(1,128)}, f32[1,512]{1,0:T(1,128)S(1)}, u32[]{:S(2)}) copy-start(f32[1,512]{1,0:T(1,128)S(1)} %get-tuple-element.616) | copy-start | bytes 6148
  19.3 9.0 %copy-start.21 = (f32[1,512]{1,0:T(1,128)}, f32[1,512]{1,0:T(1,128)S(1)}, u32[]{:S(2)}) copy-start(f32[1,512]{1,0:T(1,128)S(1)} %get-tuple-element.617) | copy-start | bytes 6148
  19.3 9.0 %copy-start.23 = (f32[1,512]{1,0:T(1,128)}, f32[1,512]{1,0:T(1,128)S(1)}, u32[]{:S(2)}) copy-start(f32[1,512]{1,0:T(1,128)S(1)} %get-tuple-element.618) | copy-start | bytes 6148
  19.4 9.0 %copy-start.25 = (f32[1,512]{1,0:T(1,128)}, f32[1,512]{1,0:T(1,128)S(1)}, u32[]{:S(2)}) copy-start(f32[1,512]{1,0:T(1,128)S(1)} %get-tuple-element.619) | copy-start | bytes 6148
  25.8 230.6 %copy-start.17 = (f32[512]{0:T(512)}, f32[512]{0:T(512)S(1)}, u32[]{:S(2)}) copy-start(f32[512]{0:T(512)S(1)} %mul.562) | copy-start | bytes 6148
  30.4 226.0 %copy-start = (f32[512,512]{0,1:T(8,128)}, f32[512,512]{0,1:T(8,128)S(1)}, u32[]{:S(2)}) copy-start(f32[512,512]{0,1:T(8,128)S(1)} %get-tuple-element.604) | copy-start | bytes 3145732
  35.7 7.2 %collective-permute-start = (f32[8,64,128]{2,1,0:T(8,128)S(1)}, f32[8,64,128]{2,1,0:T(8,128)S(1)}, u32[]{:S(2)}, u32[]{:S(2)}) collective-permute-start(f32[8,64,128]{2,1,0:T(8,128)S(1)} %multiply_add_fusion.6), channel_id=1, source_target_pairs={{0,16},{16,32},{32,48},{48,64},{64,80},{80,96},{96,112},{112,128},... | collective-permute-start | bytes 786440 | tf_op jit(solution)/shard_map/while/body/eval_jaxpr/ppermute | solution.py:16
  43.0 7.7 %collective-permute-start = (f32[8,64,128]{2,1,0:T(8,128)S(1)}, f32[8,64,128]{2,1,0:T(8,128)S(1)}, u32[]{:S(2)}, u32[]{:S(2)}) collective-permute-start(f32[8,64,128]{2,1,0:T(8,128)S(1)} %multiply_add_fusion.6), channel_id=1, source_target_pairs={{0,16},{16,32},{32,48},{48,64},{64,80},{80,96},{96,112},{112,128},... | collective-permute-start | bytes 786440 | tf_op jit(solution)/shard_map/while/body/eval_jaxpr/ppermute | solution.py:16
  50.8 7.7 %collective-permute-start = (f32[8,64,128]{2,1,0:T(8,128)S(1)}, f32[8,64,128]{2,1,0:T(8,128)S(1)}, u32[]{:S(2)}, u32[]{:S(2)}) collective-permute-start(f32[8,64,128]{2,1,0:T(8,128)S(1)} %multiply_add_fusion.6), channel_id=1, source_target_pairs={{0,16},{16,32},{32,48},{48,64},{64,80},{80,96},{96,112},{112,128},... | collective-permute-start | bytes 786440 | tf_op jit(solution)/shard_map/while/body/eval_jaxpr/ppermute | solution.py:16
  58.6 7.7 %collective-permute-start = (f32[8,64,128]{2,1,0:T(8,128)S(1)}, f32[8,64,128]{2,1,0:T(8,128)S(1)}, u32[]{:S(2)}, u32[]{:S(2)}) collective-permute-start(f32[8,64,128]{2,1,0:T(8,128)S(1)} %multiply_add_fusion.6), channel_id=1, source_target_pairs={{0,16},{16,32},{32,48},{48,64},{64,80},{80,96},{96,112},{112,128},... | collective-permute-start | bytes 786440 | tf_op jit(solution)/shard_map/while/body/eval_jaxpr/ppermute | solution.py:16
  66.4 7.7 %collective-permute-start = (f32[8,64,128]{2,1,0:T(8,128)S(1)}, f32[8,64,128]{2,1,0:T(8,128)S(1)}, u32[]{:S(2)}, u32[]{:S(2)}) collective-permute-start(f32[8,64,128]{2,1,0:T(8,128)S(1)} %multiply_add_fusion.6), channel_id=1, source_target_pairs={{0,16},{16,32},{32,48},{48,64},{64,80},{80,96},{96,112},{112,128},... | collective-permute-start | bytes 786440 | tf_op jit(solution)/shard_map/while/body/eval_jaxpr/ppermute | solution.py:16
  74.2 7.7 %collective-permute-start = (f32[8,64,128]{2,1,0:T(8,128)S(1)}, f32[8,64,128]{2,1,0:T(8,128)S(1)}, u32[]{:S(2)}, u32[]{:S(2)}) collective-permute-start(f32[8,64,128]{2,1,0:T(8,128)S(1)} %multiply_add_fusion.6), channel_id=1, source_target_pairs={{0,16},{16,32},{32,48},{48,64},{64,80},{80,96},{96,112},{112,128},... | collective-permute-start | bytes 786440 | tf_op jit(solution)/shard_map/while/body/eval_jaxpr/ppermute | solution.py:16
  82.0 7.7 %collective-permute-start = (f32[8,64,128]{2,1,0:T(8,128)S(1)}, f32[8,64,128]{2,1,0:T(8,128)S(1)}, u32[]{:S(2)}, u32[]{:S(2)}) collective-permute-start(f32[8,64,128]{2,1,0:T(8,128)S(1)} %multiply_add_fusion.6), channel_id=1, source_target_pairs={{0,16},{16,32},{32,48},{48,64},{64,80},{80,96},{96,112},{112,128},... | collective-permute-start | bytes 786440 | tf_op jit(solution)/shard_map/while/body/eval_jaxpr/ppermute | solution.py:16
  89.8 7.7 %collective-permute-start = (f32[8,64,128]{2,1,0:T(8,128)S(1)}, f32[8,64,128]{2,1,0:T(8,128)S(1)}, u32[]{:S(2)}, u32[]{:S(2)}) collective-permute-start(f32[8,64,128]{2,1,0:T(8,128)S(1)} %multiply_add_fusion.6), channel_id=1, source_target_pairs={{0,16},{16,32},{32,48},{48,64},{64,80},{80,96},{96,112},{112,128},... | collective-permute-start | bytes 786440 | tf_op jit(solution)/shard_map/while/body/eval_jaxpr/ppermute | solution.py:16
  97.5 7.7 %collective-permute-start = (f32[8,64,128]{2,1,0:T(8,128)S(1)}, f32[8,64,128]{2,1,0:T(8,128)S(1)}, u32[]{:S(2)}, u32[]{:S(2)}) collective-permute-start(f32[8,64,128]{2,1,0:T(8,128)S(1)} %multiply_add_fusion.6), channel_id=1, source_target_pairs={{0,16},{16,32},{32,48},{48,64},{64,80},{80,96},{96,112},{112,128},... | collective-permute-start | bytes 786440 | tf_op jit(solution)/shard_map/while/body/eval_jaxpr/ppermute | solution.py:16
  105.3 7.7 %collective-permute-start = (f32[8,64,128]{2,1,0:T(8,128)S(1)}, f32[8,64,128]{2,1,0:T(8,128)S(1)}, u32[]{:S(2)}, u32[]{:S(2)}) collective-permute-start(f32[8,64,128]{2,1,0:T(8,128)S(1)} %multiply_add_fusion.6), channel_id=1, source_target_pairs={{0,16},{16,32},{32,48},{48,64},{64,80},{80,96},{96,112},{112,128},... | collective-permute-start | bytes 786440 | tf_op jit(solution)/shard_map/while/body/eval_jaxpr/ppermute | solution.py:16
  113.1 7.7 %collective-permute-start = (f32[8,64,128]{2,1,0:T(8,128)S(1)}, f32[8,64,128]{2,1,0:T(8,128)S(1)}, u32[]{:S(2)}, u32[]{:S(2)}) collective-permute-start(f32[8,64,128]{2,1,0:T(8,128)S(1)} %multiply_add_fusion.6), channel_id=1, source_target_pairs={{0,16},{16,32},{32,48},{48,64},{64,80},{80,96},{96,112},{112,128},... | collective-permute-start | bytes 786440 | tf_op jit(solution)/shard_map/while/body/eval_jaxpr/ppermute | solution.py:16
  120.9 7.7 %collective-permute-start = (f32[8,64,128]{2,1,0:T(8,128)S(1)}, f32[8,64,128]{2,1,0:T(8,128)S(1)}, u32[]{:S(2)}, u32[]{:S(2)}) collective-permute-start(f32[8,64,128]{2,1,0:T(8,128)S(1)} %multiply_add_fusion.6), channel_id=1, source_target_pairs={{0,16},{16,32},{32,48},{48,64},{64,80},{80,96},{96,112},{112,128},... | collective-permute-start | bytes 786440 | tf_op jit(solution)/shard_map/while/body/eval_jaxpr/ppermute | solution.py:16
  128.7 7.7 %collective-permute-start = (f32[8,64,128]{2,1,0:T(8,128)S(1)}, f32[8,64,128]{2,1,0:T(8,128)S(1)}, u32[]{:S(2)}, u32[]{:S(2)}) collective-permute-start(f32[8,64,128]{2,1,0:T(8,128)S(1)} %multiply_add_fusion.6), channel_id=1, source_target_pairs={{0,16},{16,32},{32,48},{48,64},{64,80},{80,96},{96,112},{112,128},... | collective-permute-start | bytes 786440 | tf_op jit(solution)/shard_map/while/body/eval_jaxpr/ppermute | solution.py:16
  136.5 7.7 %collective-permute-start = (f32[8,64,128]{2,1,0:T(8,128)S(1)}, f32[8,64,128]{2,1,0:T(8,128)S(1)}, u32[]{:S(2)}, u32[]{:S(2)}) collective-permute-start(f32[8,64,128]{2,1,0:T(8,128)S(1)} %multiply_add_fusion.6), channel_id=1, source_target_pairs={{0,16},{16,32},{32,48},{48,64},{64,80},{80,96},{96,112},{112,128},... | collective-permute-start | bytes 786440 | tf_op jit(solution)/shard_map/while/body/eval_jaxpr/ppermute | solution.py:16
  144.3 7.7 %collective-permute-start = (f32[8,64,128]{2,1,0:T(8,128)S(1)}, f32[8,64,128]{2,1,0:T(8,128)S(1)}, u32[]{:S(2)}, u32[]{:S(2)}) collective-permute-start(f32[8,64,128]{2,1,0:T(8,128)S(1)} %multiply_add_fusion.6), channel_id=1, source_target_pairs={{0,16},{16,32},{32,48},{48,64},{64,80},{80,96},{96,112},{112,128},... | collective-permute-start | bytes 786440 | tf_op jit(solution)/shard_map/while/body/eval_jaxpr/ppermute | solution.py:16
  191.0 34.5 %copy-start.37 = (f32[512]{0:T(512)S(1)}, f32[512]{0:T(512)}, u32[]{:S(2)}) copy-start(f32[512]{0:T(512)} %param.32) | copy-start | bytes 6148
  192.0 64.4 %copy-start.5 = (f32[512,512]{0,1:T(8,128)}, f32[512,512]{0,1:T(8,128)S(1)}, u32[]{:S(2)}) copy-start(f32[512,512]{0,1:T(8,128)S(1)} %get-tuple-element.602) | copy-start | bytes 3145732
  263.6 22.3 %collective-permute-start.1 = (f32[8,64,128]{2,1,0:T(8,128)S(1)}, f32[8,64,128]{2,1,0:T(8,128)S(1)}, u32[]{:S(2)}, u32[]{:S(2)}) collective-permute-start(f32[8,64,128]{2,1,0:T(8,128)S(1)} %multiply_add_fusion.7), channel_id=1, source_target_pairs={{16,0},{32,16},{48,32},{64,48},{80,64},{96,80},{112,96},{128,112},... | collective-permute-start | bytes 786440 | tf_op jit(solution)/shard_map/while/body/eval_jaxpr/ppermute | solution.py:16
  286.0 7.7 %collective-permute-start.1 = (f32[8,64,128]{2,1,0:T(8,128)S(1)}, f32[8,64,128]{2,1,0:T(8,128)S(1)}, u32[]{:S(2)}, u32[]{:S(2)}) collective-permute-start(f32[8,64,128]{2,1,0:T(8,128)S(1)} %multiply_add_fusion.7), channel_id=1, source_target_pairs={{16,0},{32,16},{48,32},{64,48},{80,64},{96,80},{112,96},{128,112},... | collective-permute-start | bytes 786440 | tf_op jit(solution)/shard_map/while/body/eval_jaxpr/ppermute | solution.py:16
  293.8 7.7 %collective-permute-start.1 = (f32[8,64,128]{2,1,0:T(8,128)S(1)}, f32[8,64,128]{2,1,0:T(8,128)S(1)}, u32[]{:S(2)}, u32[]{:S(2)}) collective-permute-start(f32[8,64,128]{2,1,0:T(8,128)S(1)} %multiply_add_fusion.7), channel_id=1, source_target_pairs={{16,0},{32,16},{48,32},{64,48},{80,64},{96,80},{112,96},{128,112},... | collective-permute-start | bytes 786440 | tf_op jit(solution)/shard_map/while/body/eval_jaxpr/ppermute | solution.py:16
  301.6 7.7 %collective-permute-start.1 = (f32[8,64,128]{2,1,0:T(8,128)S(1)}, f32[8,64,128]{2,1,0:T(8,128)S(1)}, u32[]{:S(2)}, u32[]{:S(2)}) collective-permute-start(f32[8,64,128]{2,1,0:T(8,128)S(1)} %multiply_add_fusion.7), channel_id=1, source_target_pairs={{16,0},{32,16},{48,32},{64,48},{80,64},{96,80},{112,96},{128,112},... | collective-permute-start | bytes 786440 | tf_op jit(solution)/shard_map/while/body/eval_jaxpr/ppermute | solution.py:16
  309.3 9.7 %collective-permute-start.1 = (f32[8,64,128]{2,1,0:T(8,128)S(1)}, f32[8,64,128]{2,1,0:T(8,128)S(1)}, u32[]{:S(2)}, u32[]{:S(2)}) collective-permute-start(f32[8,64,128]{2,1,0:T(8,128)S(1)} %multiply_add_fusion.7), channel_id=1, source_target_pairs={{16,0},{32,16},{48,32},{64,48},{80,64},{96,80},{112,96},{128,112},... | collective-permute-start | bytes 786440 | tf_op jit(solution)/shard_map/while/body/eval_jaxpr/ppermute | solution.py:16
  319.2 7.7 %collective-permute-start.1 = (f32[8,64,128]{2,1,0:T(8,128)S(1)}, f32[8,64,128]{2,1,0:T(8,128)S(1)}, u32[]{:S(2)}, u32[]{:S(2)}) collective-permute-start(f32[8,64,128]{2,1,0:T(8,128)S(1)} %multiply_add_fusion.7), channel_id=1, source_target_pairs={{16,0},{32,16},{48,32},{64,48},{80,64},{96,80},{112,96},{128,112},... | collective-permute-start | bytes 786440 | tf_op jit(solution)/shard_map/while/body/eval_jaxpr/ppermute | solution.py:16
  327.0 10.7 %collective-permute-start.1 = (f32[8,64,128]{2,1,0:T(8,128)S(1)}, f32[8,64,128]{2,1,0:T(8,128)S(1)}, u32[]{:S(2)}, u32[]{:S(2)}) collective-permute-start(f32[8,64,128]{2,1,0:T(8,128)S(1)} %multiply_add_fusion.7), channel_id=1, source_target_pairs={{16,0},{32,16},{48,32},{64,48},{80,64},{96,80},{112,96},{128,112},... | collective-permute-start | bytes 786440 | tf_op jit(solution)/shard_map/while/body/eval_jaxpr/ppermute | solution.py:16
  337.8 8.9 %collective-permute-start.1 = (f32[8,64,128]{2,1,0:T(8,128)S(1)}, f32[8,64,128]{2,1,0:T(8,128)S(1)}, u32[]{:S(2)}, u32[]{:S(2)}) collective-permute-start(f32[8,64,128]{2,1,0:T(8,128)S(1)} %multiply_add_fusion.7), channel_id=1, source_target_pairs={{16,0},{32,16},{48,32},{64,48},{80,64},{96,80},{112,96},{128,112},... | collective-permute-start | bytes 786440 | tf_op jit(solution)/shard_map/while/body/eval_jaxpr/ppermute | solution.py:16
  346.8 8.9 %collective-permute-start.1 = (f32[8,64,128]{2,1,0:T(8,128)S(1)}, f32[8,64,128]{2,1,0:T(8,128)S(1)}, u32[]{:S(2)}, u32[]{:S(2)}) collective-permute-start(f32[8,64,128]{2,1,0:T(8,128)S(1)} %multiply_add_fusion.7), channel_id=1, source_target_pairs={{16,0},{32,16},{48,32},{64,48},{80,64},{96,80},{112,96},{128,112},... | collective-permute-start | bytes 786440 | tf_op jit(solution)/shard_map/while/body/eval_jaxpr/ppermute | solution.py:16
  355.8 8.9 %collective-permute-start.1 = (f32[8,64,128]{2,1,0:T(8,128)S(1)}, f32[8,64,128]{2,1,0:T(8,128)S(1)}, u32[]{:S(2)}, u32[]{:S(2)}) collective-permute-start(f32[8,64,128]{2,1,0:T(8,128)S(1)} %multiply_add_fusion.7), channel_id=1, source_target_pairs={{16,0},{32,16},{48,32},{64,48},{80,64},{96,80},{112,96},{128,112},... | collective-permute-start | bytes 786440 | tf_op jit(solution)/shard_map/while/body/eval_jaxpr/ppermute | solution.py:16
  364.8 8.9 %collective-permute-start.1 = (f32[8,64,128]{2,1,0:T(8,128)S(1)}, f32[8,64,128]{2,1,0:T(8,128)S(1)}, u32[]{:S(2)}, u32[]{:S(2)}) collective-permute-start(f32[8,64,128]{2,1,0:T(8,128)S(1)} %multiply_add_fusion.7), channel_id=1, source_target_pairs={{16,0},{32,16},{48,32},{64,48},{80,64},{96,80},{112,96},{128,112},... | collective-permute-start | bytes 786440 | tf_op jit(solution)/shard_map/while/body/eval_jaxpr/ppermute | solution.py:16
  373.8 8.9 %collective-permute-start.1 = (f32[8,64,128]{2,1,0:T(8,128)S(1)}, f32[8,64,128]{2,1,0:T(8,128)S(1)}, u32[]{:S(2)}, u32[]{:S(2)}) collective-permute-start(f32[8,64,128]{2,1,0:T(8,128)S(1)} %multiply_add_fusion.7), channel_id=1, source_target_pairs={{16,0},{32,16},{48,32},{64,48},{80,64},{96,80},{112,96},{128,112},... | collective-permute-start | bytes 786440 | tf_op jit(solution)/shard_map/while/body/eval_jaxpr/ppermute | solution.py:16
  382.8 8.9 %collective-permute-start.1 = (f32[8,64,128]{2,1,0:T(8,128)S(1)}, f32[8,64,128]{2,1,0:T(8,128)S(1)}, u32[]{:S(2)}, u32[]{:S(2)}) collective-permute-start(f32[8,64,128]{2,1,0:T(8,128)S(1)} %multiply_add_fusion.7), channel_id=1, source_target_pairs={{16,0},{32,16},{48,32},{64,48},{80,64},{96,80},{112,96},{128,112},... | collective-permute-start | bytes 786440 | tf_op jit(solution)/shard_map/while/body/eval_jaxpr/ppermute | solution.py:16
  391.8 8.9 %collective-permute-start.1 = (f32[8,64,128]{2,1,0:T(8,128)S(1)}, f32[8,64,128]{2,1,0:T(8,128)S(1)}, u32[]{:S(2)}, u32[]{:S(2)}) collective-permute-start(f32[8,64,128]{2,1,0:T(8,128)S(1)} %multiply_add_fusion.7), channel_id=1, source_target_pairs={{16,0},{32,16},{48,32},{64,48},{80,64},{96,80},{112,96},{128,112},... | collective-permute-start | bytes 786440 | tf_op jit(solution)/shard_map/while/body/eval_jaxpr/ppermute | solution.py:16
  400.8 8.9 %collective-permute-start.1 = (f32[8,64,128]{2,1,0:T(8,128)S(1)}, f32[8,64,128]{2,1,0:T(8,128)S(1)}, u32[]{:S(2)}, u32[]{:S(2)}) collective-permute-start(f32[8,64,128]{2,1,0:T(8,128)S(1)} %multiply_add_fusion.7), channel_id=1, source_target_pairs={{16,0},{32,16},{48,32},{64,48},{80,64},{96,80},{112,96},{128,112},... | collective-permute-start | bytes 786440 | tf_op jit(solution)/shard_map/while/body/eval_jaxpr/ppermute | solution.py:16
  501.2 6.1 collective-permute-start.5
  503.2 5.2 copy-start.3
  508.4 6.0 copy-start.16
  508.5 6.0 copy-start.27
  508.5 6.0 copy-start.28
  508.5 6.0 copy-start.42
  508.5 6.8 %copy-start.44 = (f32[8]{0:T(128)S(1)}, f32[8]{0:T(128)}, u32[]{:S(2)}) copy-start(f32[8]{0:T(128)} %param.28) | copy-start | bytes 100
  508.5 6.8 %copy-start.39 = (f32[512]{0:T(512)S(1)}, f32[512]{0:T(512)}, u32[]{:S(2)}) copy-start(f32[512]{0:T(512)} %get-tuple-element.597) | copy-start | bytes 6148
  508.5 7.0 %copy-start.40 = (f32[512]{0:T(512)S(1)}, f32[512]{0:T(512)}, u32[]{:S(2)}) copy-start(f32[512]{0:T(512)} %get-tuple-element.495) | copy-start | bytes 6148
  512.3 67.9 %copy-start.9 = (bf16[512,512]{0,1:T(8,128)(2,1)S(1)}, bf16[512,512]{0,1:T(8,128)(2,1)}, u32[]{:S(2)}) copy-start(bf16[512,512]{0,1:T(8,128)(2,1)} %get-tuple-element.609) | copy-start | bytes 1572868
  512.4 149.7 %collective-permute-start.4 = (f32[3,512]{0,1:T(8,128)S(1)}, f32[3,512]{0,1:T(8,128)S(1)}, u32[]{:S(2)}, u32[]{:S(2)}) collective-permute-start(f32[3,512]{0,1:T(8,128)S(1)} %slice.175), channel_id=1, source_target_pairs={{16,0},{32,16},{48,32},{64,48},{80,64},{96,80},{112,96},{128,112},... | collective-permute-start | bytes 18440 | tf_op jit(solution)/shard_map/ppermute | solution.py:16
  578.2 83.8 %copy-start.20 = (f32[1,512]{1,0:T(1,128)S(1)}, f32[1,512]{1,0:T(1,128)}, u32[]{:S(2)}) copy-start(f32[1,512]{1,0:T(1,128)} %copy-done.19) | copy-start | bytes 6148
  578.2 83.8 %copy-start.22 = (f32[1,512]{1,0:T(1,128)S(1)}, f32[1,512]{1,0:T(1,128)}, u32[]{:S(2)}) copy-start(f32[1,512]{1,0:T(1,128)} %copy-done.21) | copy-start | bytes 6148
  578.2 83.8 %copy-start.24 = (f32[1,512]{1,0:T(1,128)S(1)}, f32[1,512]{1,0:T(1,128)}, u32[]{:S(2)}) copy-start(f32[1,512]{1,0:T(1,128)} %copy-done.23) | copy-start | bytes 6148
  578.2 83.9 %copy-start.26 = (f32[1,512]{1,0:T(1,128)S(1)}, f32[1,512]{1,0:T(1,128)}, u32[]{:S(2)}) copy-start(f32[1,512]{1,0:T(1,128)} %copy-done.25) | copy-start | bytes 6148
  (16 other events, 50.0 us)
Sparse Core Ops, SparseCore 0:
  508.5 93.7 reduce-scatter.1
where the time goes:
time: 679 us; the launch traced here: 673 us
  blocking collectives  206 us (30%)
  waiting for transfers between devices  159 us (23%)
  starting transfers between devices  115 us (17%)
  local copies, waits for them, and re-layouts  93.2 us (14%)
  other arithmetic  42.8 us (6%)
  matrix products  41.9 us (6%)
  between operations  14.8 us (2%)
    ppermute x34, waiting for transfers between devices, passed_along(): return lax.ppermute(block, axis, route)  159 us
    ppermute x34, starting transfers between devices, passed_along(): return lax.ppermute(block, axis, route)  115 us
    psum x1, blocking collectives, local(): grad_convbc = lax.psum(grad_convbc_part, ('ctx', 'head'))  80.8 us
    psum x1, blocking collectives, local(): lax.psum((grad_alog_part, grad_skip_part, grad_convx_part, grad_gain_part...  62.7 us
    psum x2, blocking collectives, local(): lax.psum((jnp.sum(gated_out * gated_out, axis=1), jnp.sum(scaled_grad * g...  62.4 us
    dynamic_update_slice x8, local copies, waits for them, and re-layouts, local(): lax.map(forward_block, (x_blocks, b_blocks, c_blocks, d_blocks, cum_block...  48.2 us
  transfers between devices with their start and end apart: 35, of which 31 were waited for; matrix products, arithmetic and copies ran while one was open for 4% of the time, Pallas kernels for 0%

commit v1 on v0

--- a/solution.py
+++ b/solution.py
@@ -2,6 +2,7 @@
 import jax.numpy as jnp
 from jax import lax
 from jax.sharding import PartitionSpec as P
+from jax.lax import all_gather
 
 HEADS = 128
 HEAD_DIM = 64
@@ -223,7 +224,7 @@
     grad_alog, grad_dskip, grad_convx, grad_gain = lax.psum(
         (grad_alog_part, grad_skip_part, grad_convx_part, grad_gain_part), "ctx"
     )
-    grad_convbc = lax.psum(grad_convbc_part, ("ctx", "head"))
+    grad_convbc = jnp.sum(all_gather(grad_convbc_part, axis_name=("ctx", "head")), 0)
     return (
         y_out,
         grad_x,

time: 679 us -> 650 us (0.957)
  blocking collectives: 206 us -> 125 us
  waiting for transfers between devices: 159 us -> 209 us
    psum x1 -> x0, blocking collectives: 80.8 us -> none  [local(): grad_convbc = lax.psum(grad_convbc_part, ('ctx', 'head'))]
    all_gather x0 -> x1, waiting for transfers between devices: none -> 29.8 us  [local(): all_gather(grad_convbc_part, axis_name=('ctx', 'head'))]
    reduce_scatter x1, waiting for transfers between devices: 0.01 us -> 19.7 us  [local(): shares = lax.psum_scatter(bc_back, 'head', scatter_dimension=0, tiled=True)]
  transfers between devices with their start and end apart: 35 -> 36, of which waited for: 31 -> 33; matrix products, arithmetic and copies ran while one was open for 4% -> 3% of each run, Pallas kernels for 0% -> 0%
where the time goes in v1:
time: 650 us; the launch traced here: 644 us
  waiting for transfers between devices  209 us (32%)
  blocking collectives  125 us (19%)
  starting transfers between devices  115 us (18%)
  local copies, waits for them, and re-layouts  92.6 us (14%)
  other arithmetic  43.1 us (7%)
  matrix products  41.9 us (6%)
  between operations  16.2 us (2%)
    ppermute x34, waiting for transfers between devices, passed_along(): return lax.ppermute(block, axis, route)  160 us
    ppermute x34, starting transfers between devices, passed_along(): return lax.ppermute(block, axis, route)  115 us
    psum x1, blocking collectives, local(): lax.psum((grad_alog_part, grad_skip_part, grad_convx_part, grad_gain_part...  62.8 us
    psum x2, blocking collectives, local(): lax.psum((jnp.sum(gated_out * gated_out, axis=1), jnp.sum(scaled_grad * g...  62.4 us
    dynamic_update_slice x8, local copies, waits for them, and re-layouts, local(): lax.map(forward_block, (x_blocks, b_blocks, c_blocks, d_blocks, cum_block...  48.2 us
    all_gather x1, waiting for transfers between devices, local(): all_gather(grad_convbc_part, axis_name=('ctx', 'head'))  29.8 us
    reduce_scatter x1, waiting for transfers between devices, local(): shares = lax.psum_scatter(bc_back, 'head', scatter_dimension=0, tiled=True)  19.7 us
  transfers between devices with their start and end apart: 36, of which 33 were waited for; matrix products, arithmetic and copies ran while one was open for 3% of the time, Pallas kernels for 0%

profile of v1, /device:TPU:1, one launch (start us, length us, event | category | flops | bytes accessed | tf_op | source)
XLA Modules:
  0.0 643.9 jit_solution(3535077294561585186)
XLA Ops:
  9.0 4.9 collective-permute-start.2
  36.4 116.3 %while.77 = (s32[]{:T(128)}, f32[8,64,128]{2,1,0:T(8,128)S(1)}, f32[8]{0:T(128)S(1)}, f32[8,64,128]{2,1,0:T(8,128)S(1)}, s32[]{:T(128)}) while((s32[]{:T(128)}, f32[8,64,128]{2,1,0:T(8,128)S(1)}, f32[8]{0:T(128)S(1)}, f32[8,64,128]{2,1,0:T(8,128)S(1)}, s32[]{:T(128)}) %tuple.173), condition=%wide.region_7.8_spmd, body=%wide.region_6.7_spmd.sunk | while | flops 131074 | bytes 1835141 | solution.py:113
  36.5 3.9 collective-permute-start
  40.5 3.3 collective-permute-done
  43.9 4.4 collective-permute-start
  48.3 3.3 collective-permute-done
  51.7 4.4 collective-permute-start
  56.1 3.3 collective-permute-done
  59.4 4.4 collective-permute-start
  67.2 4.4 collective-permute-start
  71.6 3.3 collective-permute-done
  75.0 4.4 collective-permute-start
  79.4 3.3 collective-permute-done
  82.8 4.4 collective-permute-start
  87.2 3.3 collective-permute-done
  90.6 4.4 collective-permute-start
  98.4 4.4 collective-permute-start
  106.2 4.4 collective-permute-start
  110.6 3.3 collective-permute-done
  113.9 4.4 collective-permute-start
  118.3 3.3 collective-permute-done
  121.7 4.4 collective-permute-start
  126.1 3.3 collective-permute-done
  129.5 4.4 collective-permute-start
  137.3 4.4 collective-permute-start
  141.7 3.3 collective-permute-done
  145.1 4.4 collective-permute-start
  149.5 3.3 collective-permute-done
  154.3 36.2 %while.78 = (s32[]{:T(128)}, f32[2,256,8,64]{1,0,3,2:T(2,128)}, f32[2,256,8,64]{1,3,2,0:T(8,128)}, f32[2,256,128]{2,1,0:T(8,128)S(1)}, f32[2,256,128]{2,1,0:T(8,...) while((s32[]{:T(128)}, f32[2,256,8,64]{1,0,3,2:T(2,128)}, ...), condition=%wide.region_9.10_spmd, body=%wide.region_8.9_spmd.sunk | while | flops 707592192 | bytes 5580925 | solution.py:127
  156.1 3.6 fusion.217
  160.8 11.5 %dynamic_update_slice.48 = f32[2,256,8,64]{1,0,3,2:T(2,128)} dynamic-update-slice(f32[2,256,8,64]{1,0,3,2:T(2,128)} %get-tuple-element.953, f32[1,256,8,64]{1,0,3,2:T(1,128)S(1)} %copy.219, s32[]{:T(128)S(6)} %copy.255, s32[]{:T(128)} %constant.125.clone.1..sunk, s32[]{:T(128)} %constant.125.clone.1..sunk, s32[]{:T(128)} %constant.125.clone.1..sunk) | dynamic-update-slice | bytes 1048580 | tf_op jit(solution)/shard_map/while/body/jit(dynamic_update_index_in_dim)/dynamic_update_slice | solution.py:127
  174.2 3.6 fusion.217
  178.9 11.5 %dynamic_update_slice.48 = f32[2,256,8,64]{1,0,3,2:T(2,128)} dynamic-update-slice(f32[2,256,8,64]{1,0,3,2:T(2,128)} %get-tuple-element.953, f32[1,256,8,64]{1,0,3,2:T(1,128)S(1)} %copy.219, s32[]{:T(128)S(6)} %copy.255, s32[]{:T(128)} %constant.125.clone.1..sunk, s32[]{:T(128)} %constant.125.clone.1..sunk, s32[]{:T(128)} %constant.125.clone.1..sunk) | dynamic-update-slice | bytes 1048580 | tf_op jit(solution)/shard_map/while/body/jit(dynamic_update_index_in_dim)/dynamic_update_slice | solution.py:127
  192.8 33.5 %psum.42 = f32[512]{0:T(512)S(1)} all-reduce(f32[512]{0:T(512)S(1)} %get-tuple-element.601), channel_id=1, replica_groups=mesh['ctx'=16,'head'=16] {'head'}, use_global_device_ids=true, to_apply=%region_11.12 | all-reduce | flops 512 | bytes 4096 | tf_op jit(solution)/shard_map/psum | solution.py:137
  228.4 28.9 %psum.43 = f32[512]{0:T(512)S(1)} all-reduce(f32[512]{0:T(512)S(1)} %get-tuple-element.496), channel_id=1, replica_groups=mesh['ctx'=16,'head'=16] {'head'}, use_global_device_ids=true, to_apply=%region_13.14 | all-reduce | flops 512 | bytes 4096 | tf_op jit(solution)/shard_map/psum | solution.py:137
  257.3 4.5 multiply_reduce_fusion.3
  264.3 146.2 %while.79 = (s32[]{:T(128)}, f32[8,64,128]{2,1,0:T(8,128)S(1)}, f32[8]{0:T(128)S(1)}, f32[8,64,128]{2,1,0:T(8,128)S(1)}, s32[]{:T(128)}) while((s32[]{:T(128)}, f32[8,64,128]{2,1,0:T(8,128)S(1)}, f32[8]{0:T(128)S(1)}, f32[8,64,128]{2,1,0:T(8,128)S(1)}, s32[]{:T(128)}) %tuple.197), condition=%wide.region_16.17_spmd, body=%wide.region_15.16_spmd.sunk | while | flops 131074 | bytes 1835141 | solution.py:159
  264.4 11.7 %collective-permute-start.1 = (f32[8,64,128]{2,1,0:T(8,128)S(1)}, f32[8,64,128]{2,1,0:T(8,128)S(1)}, u32[]{:S(2)}, u32[]{:S(2)}) collective-permute-start(f32[8,64,128]{2,1,0:T(8,128)S(1)} %multiply_add_fusion.7), channel_id=1, source_target_pairs={{16,0},{32,16},{48,32},{64,48},{80,64},{96,80},{112,96},{128,112},... | collective-permute-start | bytes 786440 | tf_op jit(solution)/shard_map/while/body/eval_jaxpr/ppermute | solution.py:17
  276.1 10.6 %collective-permute-done.1 = f32[8,64,128]{2,1,0:T(8,128)S(1)} collective-permute-done((f32[8,64,128]{2,1,0:T(8,128)S(1)}, f32[8,64,128]{2,1,0:T(8,128)S(1)}, u32[]{:S(2)}, u32[]{:S(2)}) %collective-permute-start.1) | collective-permute-done | bytes 262176 | tf_op jit(solution)/shard_map/while/body/eval_jaxpr/ppermute | solution.py:17
  288.7 5.8 collective-permute-done.1
  296.5 5.8 collective-permute-done.1
  304.3 5.8 collective-permute-done.1
  312.1 7.8 %collective-permute-done.1 = f32[8,64,128]{2,1,0:T(8,128)S(1)} collective-permute-done((f32[8,64,128]{2,1,0:T(8,128)S(1)}, f32[8,64,128]{2,1,0:T(8,128)S(1)}, u32[]{:S(2)}, u32[]{:S(2)}) %collective-permute-start.1) | collective-permute-done | bytes 262176 | tf_op jit(solution)/shard_map/while/body/eval_jaxpr/ppermute | solution.py:17
  321.9 5.8 collective-permute-done.1
  329.7 8.8 %collective-permute-done.1 = f32[8,64,128]{2,1,0:T(8,128)S(1)} collective-permute-done((f32[8,64,128]{2,1,0:T(8,128)S(1)}, f32[8,64,128]{2,1,0:T(8,128)S(1)}, u32[]{:S(2)}, u32[]{:S(2)}) %collective-permute-start.1) | collective-permute-done | bytes 262176 | tf_op jit(solution)/shard_map/while/body/eval_jaxpr/ppermute | solution.py:17
  340.5 7.0 %collective-permute-done.1 = f32[8,64,128]{2,1,0:T(8,128)S(1)} collective-permute-done((f32[8,64,128]{2,1,0:T(8,128)S(1)}, f32[8,64,128]{2,1,0:T(8,128)S(1)}, u32[]{:S(2)}, u32[]{:S(2)}) %collective-permute-start.1) | collective-permute-done | bytes 262176 | tf_op jit(solution)/shard_map/while/body/eval_jaxpr/ppermute | solution.py:17
  349.5 7.0 %collective-permute-done.1 = f32[8,64,128]{2,1,0:T(8,128)S(1)} collective-permute-done((f32[8,64,128]{2,1,0:T(8,128)S(1)}, f32[8,64,128]{2,1,0:T(8,128)S(1)}, u32[]{:S(2)}, u32[]{:S(2)}) %collective-permute-start.1) | collective-permute-done | bytes 262176 | tf_op jit(solution)/shard_map/while/body/eval_jaxpr/ppermute | solution.py:17
  358.5 7.0 %collective-permute-done.1 = f32[8,64,128]{2,1,0:T(8,128)S(1)} collective-permute-done((f32[8,64,128]{2,1,0:T(8,128)S(1)}, f32[8,64,128]{2,1,0:T(8,128)S(1)}, u32[]{:S(2)}, u32[]{:S(2)}) %collective-permute-start.1) | collective-permute-done | bytes 262176 | tf_op jit(solution)/shard_map/while/body/eval_jaxpr/ppermute | solution.py:17
  367.5 7.0 %collective-permute-done.1 = f32[8,64,128]{2,1,0:T(8,128)S(1)} collective-permute-done((f32[8,64,128]{2,1,0:T(8,128)S(1)}, f32[8,64,128]{2,1,0:T(8,128)S(1)}, u32[]{:S(2)}, u32[]{:S(2)}) %collective-permute-start.1) | collective-permute-done | bytes 262176 | tf_op jit(solution)/shard_map/while/body/eval_jaxpr/ppermute | solution.py:17
  376.5 7.0 %collective-permute-done.1 = f32[8,64,128]{2,1,0:T(8,128)S(1)} collective-permute-done((f32[8,64,128]{2,1,0:T(8,128)S(1)}, f32[8,64,128]{2,1,0:T(8,128)S(1)}, u32[]{:S(2)}, u32[]{:S(2)}) %collective-permute-start.1) | collective-permute-done | bytes 262176 | tf_op jit(solution)/shard_map/while/body/eval_jaxpr/ppermute | solution.py:17
  385.5 7.0 %collective-permute-done.1 = f32[8,64,128]{2,1,0:T(8,128)S(1)} collective-permute-done((f32[8,64,128]{2,1,0:T(8,128)S(1)}, f32[8,64,128]{2,1,0:T(8,128)S(1)}, u32[]{:S(2)}, u32[]{:S(2)}) %collective-permute-start.1) | collective-permute-done | bytes 262176 | tf_op jit(solution)/shard_map/while/body/eval_jaxpr/ppermute | solution.py:17
  394.5 7.0 %collective-permute-done.1 = f32[8,64,128]{2,1,0:T(8,128)S(1)} collective-permute-done((f32[8,64,128]{2,1,0:T(8,128)S(1)}, f32[8,64,128]{2,1,0:T(8,128)S(1)}, u32[]{:S(2)}, u32[]{:S(2)}) %collective-permute-start.1) | collective-permute-done | bytes 262176 | tf_op jit(solution)/shard_map/while/body/eval_jaxpr/ppermute | solution.py:17
  403.5 7.0 %collective-permute-done.1 = f32[8,64,128]{2,1,0:T(8,128)S(1)} collective-permute-done((f32[8,64,128]{2,1,0:T(8,128)S(1)}, f32[8,64,128]{2,1,0:T(8,128)S(1)}, u32[]{:S(2)}, u32[]{:S(2)}) %collective-permute-start.1) | collective-permute-done | bytes 262176 | tf_op jit(solution)/shard_map/while/body/eval_jaxpr/ppermute | solution.py:17
  412.2 87.2 %while.81 = (s32[]{:T(128)}, f32[2,256,8,64]{1,0,3,2:T(2,128)}, f32[2,256,128]{2,1,0:T(8,128)}, f32[2,256,128]{2,1,0:T(8,128)}, f32[2,256,8]{1,2,0:T(8,128)}, /*...) while((s32[]{:T(128)}, f32[2,256,8,64]{1,0,3,2:T(2,128)}, ...), condition=%wide.region_30.31_spmd, body=%wide.region_19.30_spmd.sunk | while | flops 1921460224 | bytes 14728557 | solution.py:198
  418.5 4.2 fusion.237
  424.1 4.3 multiply_reduce_fusion.9
  444.3 11.5 %dynamic_update_slice.53 = f32[2,256,8,64]{1,0,3,2:T(2,128)} dynamic-update-slice(f32[2,256,8,64]{1,0,3,2:T(2,128)} %get-tuple-element.1024, f32[1,256,8,64]{1,0,3,2:T(1,128)S(1)} %copy.225, s32[]{:T(128)S(6)} %copy.280, s32[]{:T(128)} %constant.125.clone.1..sunk.1, s32[]{:T(128)} %constant.125.clone.1..sunk.1, s32[]{:T(128)} %constant.125.clone.1..sunk.1) | dynamic-update-slice | bytes 1048580 | tf_op jit(solution)/shard_map/while/body/jit(dynamic_update_index_in_dim)/dynamic_update_slice | solution.py:127
  462.1 4.2 fusion.237
  467.7 4.3 multiply_reduce_fusion.9
  487.9 11.5 %dynamic_update_slice.53 = f32[2,256,8,64]{1,0,3,2:T(2,128)} dynamic-update-slice(f32[2,256,8,64]{1,0,3,2:T(2,128)} %get-tuple-element.1024, f32[1,256,8,64]{1,0,3,2:T(1,128)S(1)} %copy.225, s32[]{:T(128)S(6)} %copy.280, s32[]{:T(128)} %constant.125.clone.1..sunk.1, s32[]{:T(128)} %constant.125.clone.1..sunk.1, s32[]{:T(128)} %constant.125.clone.1..sunk.1) | dynamic-update-slice | bytes 1048580 | tf_op jit(solution)/shard_map/while/body/jit(dynamic_update_index_in_dim)/dynamic_update_slice | solution.py:127
  504.1 4.2 collective-permute-done.5
  516.2 62.8 %all-reduce = (f32[8]{0:T(128)}, f32[8]{0:T(128)}, f32[4,512]{1,0:T(4,128)}, f32[512]{0:T(512)}) all-reduce(f32[8]{0:T(128)S(1)} %negate_multiply_fusion, f32[8]{0:T(128)S(1)} %reduce_sum.234, f32[4,512]{1,0:T(4,128)S(1)} %pad_maximum_fusion.5, f32[512]{0:T(512)S(1)} %copy-done.42), channel_id=1, replica_groups=mesh['ctx'=16,'head'=16] {'ctx'}, use_global_device_ids=true, to_apply=%region_33.34 | all-reduce | flops 2576 | bytes 20608 | tf_op jit(solution)/shard_map/psum | solution.py:224
  583.5 19.7 %reduce-scatter.2.cloned.1.call-done = f32[32,256]{1,0:T(8,128)} async-done(((f32[512,256]{1,0:T(8,128)}), f32[32,256]{1,0:T(8,128)}) %reduce-scatter.2.cloned.1.call-update) | async-done | bytes 32784 | tf_op jit(solution)/shard_map/reduce_scatter | solution.py:219
  604.6 29.8 %all-gather.4.cloned.1.call-done = f32[256,4,256]{2,1,0:T(4,128)} async-done(((f32[1,4,256]{2,1,0:T(4,128)}), f32[256,4,256]{2,1,0:T(4,128)}) %all-gather.4.cloned.1.call-update) | async-done | bytes 1048592 | tf_op jit(solution)/shard_map/all_gather | solution.py:227
  (315 shorter events, 149.7 us)
Async XLA Ops:
  8.0 18.2 %copy-start.13 = (bf16[512,512]{1,0:T(8,128)(2,1)S(1)}, bf16[512,512]{1,0:T(8,128)(2,1)}, u32[]{:S(2)}) copy-start(bf16[512,512]{1,0:T(8,128)(2,1)} %param.23) | copy-start | bytes 1572868
  8.0 18.4 %copy-start.45 = (f32[8]{0:T(128)S(1)}, f32[8]{0:T(128)}, u32[]{:S(2)}) copy-start(f32[8]{0:T(128)} %param.29) | copy-start | bytes 100
  8.0 595.2 %reduce-scatter.2.cloned.1.call-start = ((), (), s32[]{:S(2)}) async-start(), calls=%async_computation.1 | async-start | bytes 557056 | tf_op jit(solution)/shard_map/reduce_scatter | solution.py:219
  8.8 17.8 %copy-start.14 = (bf16[512,512]{1,0:T(8,128)(2,1)S(1)}, bf16[512,512]{1,0:T(8,128)(2,1)}, u32[]{:S(2)}) copy-start(bf16[512,512]{1,0:T(8,128)(2,1)} %param.24) | copy-start | bytes 1572868
  9.0 20.1 %collective-permute-start.2 = (bf16[3,512]{0,1:T(8,128)(2,1)S(1)}, bf16[3,512]{0,1:T(8,128)(2,1)S(1)}, u32[]{:S(2)}, u32[]{:S(2)}) collective-permute-start(bf16[3,512]{0,1:T(8,128)(2,1)S(1)} %copy.135), channel_id=1, source_target_pairs={{0,16},{16,32},{32,48},{48,64},{64,80},{80,96},{96,112},{112,128},... | collective-permute-start | bytes 9224 | tf_op jit(solution)/shard_map/ppermute | solution.py:17
  15.8 12.9 %copy-start.12 = (bf16[512,256]{1,0:T(8,128)(2,1)}, bf16[512,256]{1,0:T(8,128)(2,1)S(1)}, u32[]{:S(2)}) copy-start(bf16[512,256]{1,0:T(8,128)(2,1)S(1)} %constant_dynamic-update-slice_fusion) | copy-start | bytes 786436
  15.8 12.9 %collective-permute-start.3 = (bf16[3,256]{1,0:T(4,128)(2,1)S(1)}, bf16[3,256]{1,0:T(4,128)(2,1)S(1)}, u32[]{:S(2)}, u32[]{:S(2)}) collective-permute-start(bf16[3,256]{1,0:T(4,128)(2,1)S(1)} %slice.165), channel_id=1, source_target_pairs={{0,16},{16,32},{32,48},{48,64},{64,80},{80,96},{96,112},{112,128},... | collective-permute-start | bytes 4616 | tf_op jit(solution)/shard_map/ppermute | solution.py:17
  18.4 3.9 copy-start.43
  19.3 9.4 %copy-start.31 = (f32[1,256]{1,0:T(1,128)}, f32[1,256]{1,0:T(1,128)S(1)}, u32[]{:S(2)}) copy-start(f32[1,256]{1,0:T(1,128)S(1)} %get-tuple-element.620) | copy-start | bytes 3076
  19.3 9.4 %copy-start.33 = (f32[1,256]{1,0:T(1,128)}, f32[1,256]{1,0:T(1,128)S(1)}, u32[]{:S(2)}) copy-start(f32[1,256]{1,0:T(1,128)S(1)} %get-tuple-element.621) | copy-start | bytes 3076
  19.3 9.4 %copy-start.35 = (f32[1,256]{1,0:T(1,128)}, f32[1,256]{1,0:T(1,128)S(1)}, u32[]{:S(2)}) copy-start(f32[1,256]{1,0:T(1,128)S(1)} %get-tuple-element.622) | copy-start | bytes 3076
  19.3 9.4 %copy-start.37 = (f32[1,256]{1,0:T(1,128)}, f32[1,256]{1,0:T(1,128)S(1)}, u32[]{:S(2)}) copy-start(f32[1,256]{1,0:T(1,128)S(1)} %get-tuple-element.623) | copy-start | bytes 3076
  20.2 9.0 %copy-start.21 = (f32[1,512]{1,0:T(1,128)}, f32[1,512]{1,0:T(1,128)S(1)}, u32[]{:S(2)}) copy-start(f32[1,512]{1,0:T(1,128)S(1)} %get-tuple-element.616) | copy-start | bytes 6148
  20.2 9.0 %copy-start.23 = (f32[1,512]{1,0:T(1,128)}, f32[1,512]{1,0:T(1,128)S(1)}, u32[]{:S(2)}) copy-start(f32[1,512]{1,0:T(1,128)S(1)} %get-tuple-element.617) | copy-start | bytes 6148
  20.2 9.0 %copy-start.25 = (f32[1,512]{1,0:T(1,128)}, f32[1,512]{1,0:T(1,128)S(1)}, u32[]{:S(2)}) copy-start(f32[1,512]{1,0:T(1,128)S(1)} %get-tuple-element.618) | copy-start | bytes 6148
  20.2 9.0 %copy-start.27 = (f32[1,512]{1,0:T(1,128)}, f32[1,512]{1,0:T(1,128)S(1)}, u32[]{:S(2)}) copy-start(f32[1,512]{1,0:T(1,128)S(1)} %get-tuple-element.619) | copy-start | bytes 6148
  26.6 230.6 %copy-start.19 = (f32[512]{0:T(512)}, f32[512]{0:T(512)S(1)}, u32[]{:S(2)}) copy-start(f32[512]{0:T(512)S(1)} %mul.562) | copy-start | bytes 6148
  31.2 226.0 %copy-start = (f32[512,512]{0,1:T(8,128)}, f32[512,512]{0,1:T(8,128)S(1)}, u32[]{:S(2)}) copy-start(f32[512,512]{0,1:T(8,128)S(1)} %get-tuple-element.604) | copy-start | bytes 3145732
  36.5 7.2 %collective-permute-start = (f32[8,64,128]{2,1,0:T(8,128)S(1)}, f32[8,64,128]{2,1,0:T(8,128)S(1)}, u32[]{:S(2)}, u32[]{:S(2)}) collective-permute-start(f32[8,64,128]{2,1,0:T(8,128)S(1)} %multiply_add_fusion.6), channel_id=1, source_target_pairs={{0,16},{16,32},{32,48},{48,64},{64,80},{80,96},{96,112},{112,128},... | collective-permute-start | bytes 786440 | tf_op jit(solution)/shard_map/while/body/eval_jaxpr/ppermute | solution.py:17
  43.9 7.7 %collective-permute-start = (f32[8,64,128]{2,1,0:T(8,128)S(1)}, f32[8,64,128]{2,1,0:T(8,128)S(1)}, u32[]{:S(2)}, u32[]{:S(2)}) collective-permute-start(f32[8,64,128]{2,1,0:T(8,128)S(1)} %multiply_add_fusion.6), channel_id=1, source_target_pairs={{0,16},{16,32},{32,48},{48,64},{64,80},{80,96},{96,112},{112,128},... | collective-permute-start | bytes 786440 | tf_op jit(solution)/shard_map/while/body/eval_jaxpr/ppermute | solution.py:17
  51.7 7.7 %collective-permute-start = (f32[8,64,128]{2,1,0:T(8,128)S(1)}, f32[8,64,128]{2,1,0:T(8,128)S(1)}, u32[]{:S(2)}, u32[]{:S(2)}) collective-permute-start(f32[8,64,128]{2,1,0:T(8,128)S(1)} %multiply_add_fusion.6), channel_id=1, source_target_pairs={{0,16},{16,32},{32,48},{48,64},{64,80},{80,96},{96,112},{112,128},... | collective-permute-start | bytes 786440 | tf_op jit(solution)/shard_map/while/body/eval_jaxpr/ppermute | solution.py:17
  59.4 7.7 %collective-permute-start = (f32[8,64,128]{2,1,0:T(8,128)S(1)}, f32[8,64,128]{2,1,0:T(8,128)S(1)}, u32[]{:S(2)}, u32[]{:S(2)}) collective-permute-start(f32[8,64,128]{2,1,0:T(8,128)S(1)} %multiply_add_fusion.6), channel_id=1, source_target_pairs={{0,16},{16,32},{32,48},{48,64},{64,80},{80,96},{96,112},{112,128},... | collective-permute-start | bytes 786440 | tf_op jit(solution)/shard_map/while/body/eval_jaxpr/ppermute | solution.py:17
  67.2 7.7 %collective-permute-start = (f32[8,64,128]{2,1,0:T(8,128)S(1)}, f32[8,64,128]{2,1,0:T(8,128)S(1)}, u32[]{:S(2)}, u32[]{:S(2)}) collective-permute-start(f32[8,64,128]{2,1,0:T(8,128)S(1)} %multiply_add_fusion.6), channel_id=1, source_target_pairs={{0,16},{16,32},{32,48},{48,64},{64,80},{80,96},{96,112},{112,128},... | collective-permute-start | bytes 786440 | tf_op jit(solution)/shard_map/while/body/eval_jaxpr/ppermute | solution.py:17
  75.0 7.7 %collective-permute-start = (f32[8,64,128]{2,1,0:T(8,128)S(1)}, f32[8,64,128]{2,1,0:T(8,128)S(1)}, u32[]{:S(2)}, u32[]{:S(2)}) collective-permute-start(f32[8,64,128]{2,1,0:T(8,128)S(1)} %multiply_add_fusion.6), channel_id=1, source_target_pairs={{0,16},{16,32},{32,48},{48,64},{64,80},{80,96},{96,112},{112,128},... | collective-permute-start | bytes 786440 | tf_op jit(solution)/shard_map/while/body/eval_jaxpr/ppermute | solution.py:17
  82.8 7.7 %collective-permute-start = (f32[8,64,128]{2,1,0:T(8,128)S(1)}, f32[8,64,128]{2,1,0:T(8,128)S(1)}, u32[]{:S(2)}, u32[]{:S(2)}) collective-permute-start(f32[8,64,128]{2,1,0:T(8,128)S(1)} %multiply_add_fusion.6), channel_id=1, source_target_pairs={{0,16},{16,32},{32,48},{48,64},{64,80},{80,96},{96,112},{112,128},... | collective-permute-start | bytes 786440 | tf_op jit(solution)/shard_map/while/body/eval_jaxpr/ppermute | solution.py:17
  90.6 7.7 %collective-permute-start = (f32[8,64,128]{2,1,0:T(8,128)S(1)}, f32[8,64,128]{2,1,0:T(8,128)S(1)}, u32[]{:S(2)}, u32[]{:S(2)}) collective-permute-start(f32[8,64,128]{2,1,0:T(8,128)S(1)} %multiply_add_fusion.6), channel_id=1, source_target_pairs={{0,16},{16,32},{32,48},{48,64},{64,80},{80,96},{96,112},{112,128},... | collective-permute-start | bytes 786440 | tf_op jit(solution)/shard_map/while/body/eval_jaxpr/ppermute | solution.py:17
  98.4 7.7 %collective-permute-start = (f32[8,64,128]{2,1,0:T(8,128)S(1)}, f32[8,64,128]{2,1,0:T(8,128)S(1)}, u32[]{:S(2)}, u32[]{:S(2)}) collective-permute-start(f32[8,64,128]{2,1,0:T(8,128)S(1)} %multiply_add_fusion.6), channel_id=1, source_target_pairs={{0,16},{16,32},{32,48},{48,64},{64,80},{80,96},{96,112},{112,128},... | collective-permute-start | bytes 786440 | tf_op jit(solution)/shard_map/while/body/eval_jaxpr/ppermute | solution.py:17
  106.2 7.7 %collective-permute-start = (f32[8,64,128]{2,1,0:T(8,128)S(1)}, f32[8,64,128]{2,1,0:T(8,128)S(1)}, u32[]{:S(2)}, u32[]{:S(2)}) collective-permute-start(f32[8,64,128]{2,1,0:T(8,128)S(1)} %multiply_add_fusion.6), channel_id=1, source_target_pairs={{0,16},{16,32},{32,48},{48,64},{64,80},{80,96},{96,112},{112,128},... | collective-permute-start | bytes 786440 | tf_op jit(solution)/shard_map/while/body/eval_jaxpr/ppermute | solution.py:17
  113.9 7.7 %collective-permute-start = (f32[8,64,128]{2,1,0:T(8,128)S(1)}, f32[8,64,128]{2,1,0:T(8,128)S(1)}, u32[]{:S(2)}, u32[]{:S(2)}) collective-permute-start(f32[8,64,128]{2,1,0:T(8,128)S(1)} %multiply_add_fusion.6), channel_id=1, source_target_pairs={{0,16},{16,32},{32,48},{48,64},{64,80},{80,96},{96,112},{112,128},... | collective-permute-start | bytes 786440 | tf_op jit(solution)/shard_map/while/body/eval_jaxpr/ppermute | solution.py:17
  121.7 7.7 %collective-permute-start = (f32[8,64,128]{2,1,0:T(8,128)S(1)}, f32[8,64,128]{2,1,0:T(8,128)S(1)}, u32[]{:S(2)}, u32[]{:S(2)}) collective-permute-start(f32[8,64,128]{2,1,0:T(8,128)S(1)} %multiply_add_fusion.6), channel_id=1, source_target_pairs={{0,16},{16,32},{32,48},{48,64},{64,80},{80,96},{96,112},{112,128},... | collective-permute-start | bytes 786440 | tf_op jit(solution)/shard_map/while/body/eval_jaxpr/ppermute | solution.py:17
  129.5 7.7 %collective-permute-start = (f32[8,64,128]{2,1,0:T(8,128)S(1)}, f32[8,64,128]{2,1,0:T(8,128)S(1)}, u32[]{:S(2)}, u32[]{:S(2)}) collective-permute-start(f32[8,64,128]{2,1,0:T(8,128)S(1)} %multiply_add_fusion.6), channel_id=1, source_target_pairs={{0,16},{16,32},{32,48},{48,64},{64,80},{80,96},{96,112},{112,128},... | collective-permute-start | bytes 786440 | tf_op jit(solution)/shard_map/while/body/eval_jaxpr/ppermute | solution.py:17
  137.3 7.7 %collective-permute-start = (f32[8,64,128]{2,1,0:T(8,128)S(1)}, f32[8,64,128]{2,1,0:T(8,128)S(1)}, u32[]{:S(2)}, u32[]{:S(2)}) collective-permute-start(f32[8,64,128]{2,1,0:T(8,128)S(1)} %multiply_add_fusion.6), channel_id=1, source_target_pairs={{0,16},{16,32},{32,48},{48,64},{64,80},{80,96},{96,112},{112,128},... | collective-permute-start | bytes 786440 | tf_op jit(solution)/shard_map/while/body/eval_jaxpr/ppermute | solution.py:17
  145.1 7.7 %collective-permute-start = (f32[8,64,128]{2,1,0:T(8,128)S(1)}, f32[8,64,128]{2,1,0:T(8,128)S(1)}, u32[]{:S(2)}, u32[]{:S(2)}) collective-permute-start(f32[8,64,128]{2,1,0:T(8,128)S(1)} %multiply_add_fusion.6), channel_id=1, source_target_pairs={{0,16},{16,32},{32,48},{48,64},{64,80},{80,96},{96,112},{112,128},... | collective-permute-start | bytes 786440 | tf_op jit(solution)/shard_map/while/body/eval_jaxpr/ppermute | solution.py:17
  191.8 34.5 %copy-start.39 = (f32[512]{0:T(512)S(1)}, f32[512]{0:T(512)}, u32[]{:S(2)}) copy-start(f32[512]{0:T(512)} %param.32) | copy-start | bytes 6148
  192.8 64.4 %copy-start.5 = (f32[512,512]{0,1:T(8,128)}, f32[512,512]{0,1:T(8,128)S(1)}, u32[]{:S(2)}) copy-start(f32[512,512]{0,1:T(8,128)S(1)} %get-tuple-element.602) | copy-start | bytes 3145732
  264.4 22.3 %collective-permute-start.1 = (f32[8,64,128]{2,1,0:T(8,128)S(1)}, f32[8,64,128]{2,1,0:T(8,128)S(1)}, u32[]{:S(2)}, u32[]{:S(2)}) collective-permute-start(f32[8,64,128]{2,1,0:T(8,128)S(1)} %multiply_add_fusion.7), channel_id=1, source_target_pairs={{16,0},{32,16},{48,32},{64,48},{80,64},{96,80},{112,96},{128,112},... | collective-permute-start | bytes 786440 | tf_op jit(solution)/shard_map/while/body/eval_jaxpr/ppermute | solution.py:17
  286.8 7.7 %collective-permute-start.1 = (f32[8,64,128]{2,1,0:T(8,128)S(1)}, f32[8,64,128]{2,1,0:T(8,128)S(1)}, u32[]{:S(2)}, u32[]{:S(2)}) collective-permute-start(f32[8,64,128]{2,1,0:T(8,128)S(1)} %multiply_add_fusion.7), channel_id=1, source_target_pairs={{16,0},{32,16},{48,32},{64,48},{80,64},{96,80},{112,96},{128,112},... | collective-permute-start | bytes 786440 | tf_op jit(solution)/shard_map/while/body/eval_jaxpr/ppermute | solution.py:17
  294.6 7.7 %collective-permute-start.1 = (f32[8,64,128]{2,1,0:T(8,128)S(1)}, f32[8,64,128]{2,1,0:T(8,128)S(1)}, u32[]{:S(2)}, u32[]{:S(2)}) collective-permute-start(f32[8,64,128]{2,1,0:T(8,128)S(1)} %multiply_add_fusion.7), channel_id=1, source_target_pairs={{16,0},{32,16},{48,32},{64,48},{80,64},{96,80},{112,96},{128,112},... | collective-permute-start | bytes 786440 | tf_op jit(solution)/shard_map/while/body/eval_jaxpr/ppermute | solution.py:17
  302.4 7.7 %collective-permute-start.1 = (f32[8,64,128]{2,1,0:T(8,128)S(1)}, f32[8,64,128]{2,1,0:T(8,128)S(1)}, u32[]{:S(2)}, u32[]{:S(2)}) collective-permute-start(f32[8,64,128]{2,1,0:T(8,128)S(1)} %multiply_add_fusion.7), channel_id=1, source_target_pairs={{16,0},{32,16},{48,32},{64,48},{80,64},{96,80},{112,96},{128,112},... | collective-permute-start | bytes 786440 | tf_op jit(solution)/shard_map/while/body/eval_jaxpr/ppermute | solution.py:17
  310.1 9.7 %collective-permute-start.1 = (f32[8,64,128]{2,1,0:T(8,128)S(1)}, f32[8,64,128]{2,1,0:T(8,128)S(1)}, u32[]{:S(2)}, u32[]{:S(2)}) collective-permute-start(f32[8,64,128]{2,1,0:T(8,128)S(1)} %multiply_add_fusion.7), channel_id=1, source_target_pairs={{16,0},{32,16},{48,32},{64,48},{80,64},{96,80},{112,96},{128,112},... | collective-permute-start | bytes 786440 | tf_op jit(solution)/shard_map/while/body/eval_jaxpr/ppermute | solution.py:17
  320.0 7.7 %collective-permute-start.1 = (f32[8,64,128]{2,1,0:T(8,128)S(1)}, f32[8,64,128]{2,1,0:T(8,128)S(1)}, u32[]{:S(2)}, u32[]{:S(2)}) collective-permute-start(f32[8,64,128]{2,1,0:T(8,128)S(1)} %multiply_add_fusion.7), channel_id=1, source_target_pairs={{16,0},{32,16},{48,32},{64,48},{80,64},{96,80},{112,96},{128,112},... | collective-permute-start | bytes 786440 | tf_op jit(solution)/shard_map/while/body/eval_jaxpr/ppermute | solution.py:17
  327.8 10.7 %collective-permute-start.1 = (f32[8,64,128]{2,1,0:T(8,128)S(1)}, f32[8,64,128]{2,1,0:T(8,128)S(1)}, u32[]{:S(2)}, u32[]{:S(2)}) collective-permute-start(f32[8,64,128]{2,1,0:T(8,128)S(1)} %multiply_add_fusion.7), channel_id=1, source_target_pairs={{16,0},{32,16},{48,32},{64,48},{80,64},{96,80},{112,96},{128,112},... | collective-permute-start | bytes 786440 | tf_op jit(solution)/shard_map/while/body/eval_jaxpr/ppermute | solution.py:17
  338.6 8.9 %collective-permute-start.1 = (f32[8,64,128]{2,1,0:T(8,128)S(1)}, f32[8,64,128]{2,1,0:T(8,128)S(1)}, u32[]{:S(2)}, u32[]{:S(2)}) collective-permute-start(f32[8,64,128]{2,1,0:T(8,128)S(1)} %multiply_add_fusion.7), channel_id=1, source_target_pairs={{16,0},{32,16},{48,32},{64,48},{80,64},{96,80},{112,96},{128,112},... | collective-permute-start | bytes 786440 | tf_op jit(solution)/shard_map/while/body/eval_jaxpr/ppermute | solution.py:17
  347.6 8.9 %collective-permute-start.1 = (f32[8,64,128]{2,1,0:T(8,128)S(1)}, f32[8,64,128]{2,1,0:T(8,128)S(1)}, u32[]{:S(2)}, u32[]{:S(2)}) collective-permute-start(f32[8,64,128]{2,1,0:T(8,128)S(1)} %multiply_add_fusion.7), channel_id=1, source_target_pairs={{16,0},{32,16},{48,32},{64,48},{80,64},{96,80},{112,96},{128,112},... | collective-permute-start | bytes 786440 | tf_op jit(solution)/shard_map/while/body/eval_jaxpr/ppermute | solution.py:17
  356.6 8.9 %collective-permute-start.1 = (f32[8,64,128]{2,1,0:T(8,128)S(1)}, f32[8,64,128]{2,1,0:T(8,128)S(1)}, u32[]{:S(2)}, u32[]{:S(2)}) collective-permute-start(f32[8,64,128]{2,1,0:T(8,128)S(1)} %multiply_add_fusion.7), channel_id=1, source_target_pairs={{16,0},{32,16},{48,32},{64,48},{80,64},{96,80},{112,96},{128,112},... | collective-permute-start | bytes 786440 | tf_op jit(solution)/shard_map/while/body/eval_jaxpr/ppermute | solution.py:17
  365.6 8.9 %collective-permute-start.1 = (f32[8,64,128]{2,1,0:T(8,128)S(1)}, f32[8,64,128]{2,1,0:T(8,128)S(1)}, u32[]{:S(2)}, u32[]{:S(2)}) collective-permute-start(f32[8,64,128]{2,1,0:T(8,128)S(1)} %multiply_add_fusion.7), channel_id=1, source_target_pairs={{16,0},{32,16},{48,32},{64,48},{80,64},{96,80},{112,96},{128,112},... | collective-permute-start | bytes 786440 | tf_op jit(solution)/shard_map/while/body/eval_jaxpr/ppermute | solution.py:17
  374.6 8.9 %collective-permute-start.1 = (f32[8,64,128]{2,1,0:T(8,128)S(1)}, f32[8,64,128]{2,1,0:T(8,128)S(1)}, u32[]{:S(2)}, u32[]{:S(2)}) collective-permute-start(f32[8,64,128]{2,1,0:T(8,128)S(1)} %multiply_add_fusion.7), channel_id=1, source_target_pairs={{16,0},{32,16},{48,32},{64,48},{80,64},{96,80},{112,96},{128,112},... | collective-permute-start | bytes 786440 | tf_op jit(solution)/shard_map/while/body/eval_jaxpr/ppermute | solution.py:17
  383.6 8.9 %collective-permute-start.1 = (f32[8,64,128]{2,1,0:T(8,128)S(1)}, f32[8,64,128]{2,1,0:T(8,128)S(1)}, u32[]{:S(2)}, u32[]{:S(2)}) collective-permute-start(f32[8,64,128]{2,1,0:T(8,128)S(1)} %multiply_add_fusion.7), channel_id=1, source_target_pairs={{16,0},{32,16},{48,32},{64,48},{80,64},{96,80},{112,96},{128,112},... | collective-permute-start | bytes 786440 | tf_op jit(solution)/shard_map/while/body/eval_jaxpr/ppermute | solution.py:17
  392.6 8.9 %collective-permute-start.1 = (f32[8,64,128]{2,1,0:T(8,128)S(1)}, f32[8,64,128]{2,1,0:T(8,128)S(1)}, u32[]{:S(2)}, u32[]{:S(2)}) collective-permute-start(f32[8,64,128]{2,1,0:T(8,128)S(1)} %multiply_add_fusion.7), channel_id=1, source_target_pairs={{16,0},{32,16},{48,32},{64,48},{80,64},{96,80},{112,96},{128,112},... | collective-permute-start | bytes 786440 | tf_op jit(solution)/shard_map/while/body/eval_jaxpr/ppermute | solution.py:17
  401.6 8.9 %collective-permute-start.1 = (f32[8,64,128]{2,1,0:T(8,128)S(1)}, f32[8,64,128]{2,1,0:T(8,128)S(1)}, u32[]{:S(2)}, u32[]{:S(2)}) collective-permute-start(f32[8,64,128]{2,1,0:T(8,128)S(1)} %multiply_add_fusion.7), channel_id=1, source_target_pairs={{16,0},{32,16},{48,32},{64,48},{80,64},{96,80},{112,96},{128,112},... | collective-permute-start | bytes 786440 | tf_op jit(solution)/shard_map/while/body/eval_jaxpr/ppermute | solution.py:17
  499.4 8.9 %copy-start.32 = (f32[1,256]{1,0:T(1,128)S(1)}, f32[1,256]{1,0:T(1,128)}, u32[]{:S(2)}) copy-start(f32[1,256]{1,0:T(1,128)} %copy-done.31) | copy-start | bytes 3076
  499.4 8.9 %copy-start.34 = (f32[1,256]{1,0:T(1,128)S(1)}, f32[1,256]{1,0:T(1,128)}, u32[]{:S(2)}) copy-start(f32[1,256]{1,0:T(1,128)} %copy-done.33) | copy-start | bytes 3076
  499.4 8.9 %copy-start.36 = (f32[1,256]{1,0:T(1,128)S(1)}, f32[1,256]{1,0:T(1,128)}, u32[]{:S(2)}) copy-start(f32[1,256]{1,0:T(1,128)} %copy-done.35) | copy-start | bytes 3076
  499.4 8.9 %copy-start.38 = (f32[1,256]{1,0:T(1,128)S(1)}, f32[1,256]{1,0:T(1,128)}, u32[]{:S(2)}) copy-start(f32[1,256]{1,0:T(1,128)} %copy-done.37) | copy-start | bytes 3076
  499.4 10.7 %copy-start.17 = (bf16[3,512]{0,1:T(8,128)(2,1)S(1)}, bf16[3,512]{0,1:T(8,128)(2,1)}, u32[]{:S(2)}) copy-start(bf16[3,512]{0,1:T(8,128)(2,1)} %copy-done.16) | copy-start | bytes 9220
  502.0 8.0 %copy-start.9 = (f32[2,256,8,64]{1,0,3,2:T(2,128)S(1)}, f32[2,256,8,64]{1,0,3,2:T(2,128)}, u32[]{:S(2)}) copy-start(f32[2,256,8,64]{1,0,3,2:T(2,128)} %get-tuple-element.310) | copy-start | bytes 3145732
  502.0 6.3 collective-permute-start.5
  509.4 125.0 %all-gather.4.cloned.1.call-start = ((), (), s32[]{:S(2)}) async-start(), calls=%async_computation.2 | async-start | bytes 1052672 | tf_op jit(solution)/shard_map/all_gather | solution.py:227
  511.6 4.4 copy-start.46
  511.6 4.4 copy-start.41
  511.7 4.6 copy-start.42
  511.7 67.3 %copy-start.11 = (bf16[512,512]{0,1:T(8,128)(2,1)S(1)}, bf16[512,512]{0,1:T(8,128)(2,1)}, u32[]{:S(2)}) copy-start(bf16[512,512]{0,1:T(8,128)(2,1)} %get-tuple-element.608) | copy-start | bytes 1572868
  513.1 67.0 %copy-start.10 = (bf16[512,512]{0,1:T(8,128)(2,1)S(1)}, bf16[512,512]{0,1:T(8,128)(2,1)}, u32[]{:S(2)}) copy-start(bf16[512,512]{0,1:T(8,128)(2,1)} %get-tuple-element.609) | copy-start | bytes 1572868
  513.1 67.9 %collective-permute-start.4 = (f32[3,512]{0,1:T(8,128)S(1)}, f32[3,512]{0,1:T(8,128)S(1)}, u32[]{:S(2)}, u32[]{:S(2)}) collective-permute-start(f32[3,512]{0,1:T(8,128)S(1)} %slice.175), channel_id=1, source_target_pairs={{16,0},{32,16},{48,32},{64,48},{80,64},{96,80},{112,96},{128,112},... | collective-permute-start | bytes 18440 | tf_op jit(solution)/shard_map/ppermute | solution.py:17
  (19 other events, 39.6 us)
Sparse Core Ops, SparseCore 0:
  509.5 93.7 reduce-scatter.1
Sparse Core Ops, SparseCore 1:
  514.1 120.2 all-gather.3
